TPU v7x, 32 devices: a whole 2x2x4 slice. The times are simulated.
32 devices in a mesh: shard: 4 (over z), ctx: 4 (over y, x), tp: 2 (over core).
Axes of the slice: x: 2, y: 2, z: 4, core: 2. Of those that a mesh axis runs over, the one named last changes fastest.
Arguments:
- hidden_in: bfloat16 [24, 680, 1024], P('shard', 'ctx'), may hold values from -6 to 6
- cond: bfloat16 [24, 1024], P('shard'), may hold values from -6 to 6
- scale_len: int32 [24, 10], P('shard'), may hold values from 1 to 256, 680 in all within a row
- ada_weight: bfloat16 [1024, 6, 1024], P('shard'), may hold values from -0.1875 to 0.1875
- ada_bias: float32 [6, 1024], replicated, may hold values from -3 to 3
- qkv_weight: bfloat16 [1024, 3, 1024], P('shard', None, 'tp'), may hold values from -0.1875 to 0.1875
- query_bias: float32 [1024], P('tp'), may hold values from -3 to 3
- value_bias: float32 [1024], P('tp'), may hold values from -3 to 3
- head_scale: float32 [16], P('tp'), may hold values from 2 to 3
- proj_weight: bfloat16 [1024, 1024], P('tp', 'shard'), may hold values from -0.5 to 0.5
- proj_bias: float32 [1024], replicated, may hold values from -2 to 2
- up_weight: bfloat16 [1024, 4096], P('shard', 'tp'), may hold values from -0.1875 to 0.1875
- up_bias: float32 [4096], P('tp'), may hold values from -3 to 3
- down_weight: bfloat16 [4096, 1024], P('tp', 'shard'), may hold values from -0.125 to 0.125
- down_bias: float32 [1024], replicated, may hold values from -2 to 2
- out_grad: bfloat16 [24, 680, 1024], P('shard', 'ctx'), may hold values from -6 to 6
Outputs:
- hidden_out: bfloat16 [24, 680, 1024], P('shard', 'ctx')
- grad_hidden: bfloat16 [24, 680, 1024], P('shard', 'ctx')
- grad_cond: float32 [24, 1024], P('shard')
- grad_ada_weight: float32 [1024, 6, 1024], P('shard')
- grad_ada_bias: float32 [6, 1024], replicated
- grad_qkv_weight: float32 [1024, 3, 1024], P('shard', None, 'tp')
- grad_query_bias: float32 [1024], P('tp')
- grad_value_bias: float32 [1024], P('tp')
- grad_head_scale: float32 [16], P('tp')
- grad_proj_weight: float32 [1024, 1024], P('tp', 'shard')
- grad_proj_bias: float32 [1024], replicated
- grad_up_weight: float32 [1024, 4096], P('shard', 'tp')
- grad_up_bias: float32 [4096], P('tp')
- grad_down_weight: float32 [4096, 1024], P('tp', 'shard')
- grad_down_bias: float32 [1024], replicated
- norm_stats: float32 [3], replicated
Inputs may be any that keep to these rules, and one draw needn't show every extreme that they name: `scale_len`: each row holds the token counts of one map's 10 scales in order; they sum to 680, and the largest in every row is 256.
All inputs are finite; a program needn't handle non-finite values.
Results may differ from a plain program's by a relative error of at most 0.03.
Values may be sent and summed in bfloat16 or wider, within the bound.
No kernel may reach another device: no remote copies, remote signals or barrier semaphores. Data moves between devices by JAX's collectives and lax.ppermute only.
A program may use at most 256 MiB of HBM per device.

v0:
```python
import jax
import jax.numpy as jnp
from jax import lax
from jax.sharding import PartitionSpec as P


def layer_norm(values):
    center = values - jnp.mean(values, axis=-1, keepdims=True)
    spread = jnp.mean(center * center, axis=-1, keepdims=True)
    return center * lax.rsqrt(spread + 1e-06)


def modulate(values, scale, shift):
    return layer_norm(values) * (1.0 + scale[:, None, :]) + shift[:, None, :]


def unit_scaled(values, gains):
    normed = values * lax.rsqrt(jnp.sum(values * values, axis=-1, keepdims=True) + 1e-06)
    return normed * jnp.exp(gains)[None, None, :, None]


def unit_plain(values):
    return values * lax.rsqrt(jnp.sum(values * values, axis=-1, keepdims=True) + 1e-06)


def gelu_tanh(values):
    return jax.nn.gelu(values, approximate=True)


def tp_sum(values):
    count = lax.axis_size("tp")
    if count != 2:
        return lax.psum(values, "tp")
    return values + lax.ppermute(values, "tp", [(0, 1), (1, 0)])


def ctx_shifts(values):
    count = lax.axis_size("ctx")
    parts = [values]
    for shift in range(1, count):
        pairs = [(i, (i + shift) % count) for i in range(count)]
        parts.append(lax.ppermute(values, "ctx", pairs))
    return jnp.stack(parts)


def ctx_return(parts):
    count = lax.axis_size("ctx")
    total = parts[0].astype(jnp.float32)
    for shift in range(1, count):
        pairs = [(i, (i - shift) % count) for i in range(count)]
        total = total + lax.ppermute(parts[shift], "ctx", pairs).astype(jnp.float32)
    return total


def group_send(values):
    count = lax.axis_size("ctx")
    me = lax.axis_index("ctx")
    parts = []
    for shift in range(count):
        block = lax.dynamic_index_in_dim(values, (me + shift) % count, axis=2, keepdims=False)
        if shift:
            pairs = [(i, (i + shift) % count) for i in range(count)]
            block = lax.ppermute(block, "ctx", pairs)
        parts.append(block)
    return jnp.stack(parts)


def group_return(parts):
    count = lax.axis_size("ctx")
    me = lax.axis_index("ctx")
    back = [parts[0]]
    for shift in range(1, count):
        pairs = [(i, (i - shift) % count) for i in range(count)]
        back.append(lax.ppermute(parts[shift], "ctx", pairs))
    stacked = jnp.stack(back)
    order = (jnp.arange(count, dtype=jnp.int32) - me) % count
    return jnp.moveaxis(jnp.take(stacked, order, axis=0), 0, 2)


def gather_axis(values, axis):
    count = lax.axis_size(axis)
    me = lax.axis_index(axis)
    parts = [values]
    for shift in range(1, count):
        pairs = [(i, (i + shift) % count) for i in range(count)]
        parts.append(lax.ppermute(values, axis, pairs))
    stacked = jnp.stack(parts)
    order = (me - jnp.arange(count, dtype=jnp.int32)) % count
    return jnp.take(stacked, order, axis=0)


def small_sum(values):
    every = gather_axis(gather_axis(values, "ctx"), "shard")
    return jnp.sum(every, axis=(0, 1))


def body(
    hidden_in,
    cond,
    scale_len,
    ada_weight,
    ada_bias,
    qkv_weight,
    query_bias,
    value_bias,
    head_scale,
    proj_weight,
    proj_bias,
    up_weight,
    up_bias,
    down_weight,
    down_bias,
    out_grad,
):
    map_count = hidden_in.shape[0]
    piece_rows = hidden_in.shape[1]
    model_width = hidden_in.shape[2]
    ctx_count = lax.axis_size("ctx")
    ctx_index = lax.axis_index("ctx")
    shard_index = lax.axis_index("shard")
    map_length = piece_rows * ctx_count
    heads_here = head_scale.shape[0]
    local_width = query_bias.shape[0]
    head_dim = local_width // heads_here
    row_count = map_count * piece_rows
    head_shape = (map_count, piece_rows, heads_here, head_dim)
    ada_rows = ada_weight.shape[0]
    shard_count = lax.axis_size("shard")
    full_qkv = lax.all_gather(qkv_weight, "shard", axis=0, tiled=True)
    packed = jnp.concatenate(
        [proj_weight.reshape(-1), up_weight.reshape(-1), down_weight.reshape(-1)]
    )
    packed_all = lax.all_gather(packed, "shard", axis=0, tiled=False)
    proj_size, up_size = (proj_weight.size, up_weight.size)
    proj_parts = packed_all[:, :proj_size].reshape((shard_count,) + proj_weight.shape)
    up_parts = packed_all[:, proj_size : proj_size + up_size].reshape(
        (shard_count,) + up_weight.shape
    )
    down_parts = packed_all[:, proj_size + up_size :].reshape((shard_count,) + down_weight.shape)
    full_proj = jnp.transpose(proj_parts, (1, 0, 2)).reshape(proj_weight.shape[0], -1)
    full_up = up_parts.reshape(-1, up_weight.shape[1])
    full_down = jnp.transpose(down_parts, (1, 0, 2)).reshape(down_weight.shape[0], -1)
    qkv_matrix = full_qkv.reshape(model_width, 3 * local_width)
    cond_wide = cond.astype(jnp.float32)
    cond_all = lax.all_gather(cond, "shard", axis=0, tiled=True).astype(jnp.float32)
    cond_in_all = jax.nn.silu(cond_all).astype(jnp.bfloat16)
    cond_cols = lax.dynamic_slice_in_dim(cond_in_all, shard_index * ada_rows, ada_rows, axis=1)
    ada_local = ada_weight.reshape(ada_rows, 6 * model_width)
    mod_partial = jnp.dot(cond_cols, ada_local, preferred_element_type=jnp.float32)
    modulation = lax.psum_scatter(mod_partial, "shard", scatter_dimension=0, tiled=True)
    modulation = modulation.reshape(map_count, 6, model_width) + ada_bias[None]
    gamma_one = modulation[:, 0]
    gamma_two = modulation[:, 1]
    scale_one = modulation[:, 2]
    scale_two = modulation[:, 3]
    shift_one = modulation[:, 4]
    shift_two = modulation[:, 5]
    stream_in = hidden_in.astype(jnp.float32)
    first_mod, first_back = jax.vjp(modulate, stream_in, scale_one, shift_one)
    attn_in = first_mod.astype(jnp.bfloat16).reshape(row_count, model_width)
    qkv = jnp.dot(attn_in, qkv_matrix, preferred_element_type=jnp.float32).reshape(
        map_count, piece_rows, 3, local_width
    )
    query = (qkv[:, :, 0] + query_bias).reshape(head_shape)
    key_raw = qkv[:, :, 1].reshape(head_shape)
    value_low = (qkv[:, :, 2] + value_bias).astype(jnp.bfloat16).reshape(head_shape)
    query_unit, query_back = jax.vjp(unit_scaled, query, head_scale)
    key_unit, key_back = jax.vjp(unit_plain, key_raw)
    query_low = query_unit.astype(jnp.bfloat16)
    key_low = key_unit.astype(jnp.bfloat16)
    group_heads = heads_here // ctx_count
    group_shape = (map_count, piece_rows, ctx_count, group_heads, head_dim)
    query_all = group_send(query_low.reshape(group_shape))
    keys_all = group_send(key_low.reshape(group_shape))
    values_all = group_send(value_low.reshape(group_shape))
    scale_ends = jnp.cumsum(scale_len, axis=1)
    owners = (ctx_index - jnp.arange(ctx_count, dtype=jnp.int32)) % ctx_count
    token_pos = owners[:, None] * piece_rows + jnp.arange(piece_rows, dtype=jnp.int32)[None, :]
    ends = scale_ends[:, None, None, :]
    visible_end = jnp.min(jnp.where(ends > token_pos[None, :, :, None], ends, map_length), axis=3)
    key_mask = token_pos[None, None, None, :, :] < visible_end[:, :, :, None, None]

    def masked_scores():
        raw_scores = jnp.einsum(
            "amqgd,bmkgd->mgaqbk", query_all, keys_all, preferred_element_type=jnp.float32
        )
        return jnp.where(key_mask[:, None], raw_scores, -1e30)

    scores = masked_scores()
    row_max = jnp.max(scores, axis=(-2, -1), keepdims=True)
    exp_scores = jnp.exp(scores - row_max)
    exp_total = jnp.sum(exp_scores, axis=(-2, -1), keepdims=True)
    log_total = row_max + jnp.log(exp_total)
    probs_low = (exp_scores / exp_total).astype(jnp.bfloat16)
    out_all = jnp.einsum(
        "mgaqbk,bmkgd->amqgd", probs_low, values_all, preferred_element_type=jnp.float32
    ).astype(jnp.bfloat16)
    heads_out = group_return(out_all).reshape(row_count, local_width)
    attn_partial = jnp.dot(heads_out, full_proj, preferred_element_type=jnp.float32)
    attn_branch = tp_sum(attn_partial).reshape(map_count, piece_rows, model_width) + proj_bias
    attn_part = gamma_one[:, None] * attn_branch
    mid_stream = stream_in + attn_part
    second_mod, second_back = jax.vjp(modulate, mid_stream, scale_two, shift_two)
    mlp_in = second_mod.astype(jnp.bfloat16).reshape(row_count, model_width)
    pre_act = jnp.dot(mlp_in, full_up, preferred_element_type=jnp.float32) + up_bias
    activation, gelu_back = jax.vjp(gelu_tanh, pre_act)
    act_low = activation.astype(jnp.bfloat16)
    mlp_partial = jnp.dot(act_low, full_down, preferred_element_type=jnp.float32)
    mlp_branch = tp_sum(mlp_partial).reshape(map_count, piece_rows, model_width) + down_bias
    mlp_part = gamma_two[:, None] * mlp_branch
    stream = mid_stream + mlp_part
    grad_top = out_grad.astype(jnp.float32)
    d_gamma_two = jnp.sum(grad_top * mlp_branch, axis=1)
    d_mlp = gamma_two[:, None] * grad_top
    d_down_bias = jnp.sum(d_mlp, axis=(0, 1))
    d_mlp_low = d_mlp.astype(jnp.bfloat16).reshape(row_count, model_width)
    g_down = jnp.einsum("rf,rd->fd", act_low, d_mlp_low, preferred_element_type=jnp.float32)
    d_act = jnp.einsum("rd,fd->rf", d_mlp_low, full_down, preferred_element_type=jnp.float32)
    (d_pre,) = gelu_back(d_act)
    d_up_bias = jnp.sum(d_pre, axis=0)
    d_pre_low = d_pre.astype(jnp.bfloat16)
    g_up = jnp.einsum("rd,rf->df", mlp_in, d_pre_low, preferred_element_type=jnp.float32)
    d_mlp_in_part = jnp.einsum("rf,df->rd", d_pre_low, full_up, preferred_element_type=jnp.float32)
    d_mlp_in = tp_sum(d_mlp_in_part).reshape(map_count, piece_rows, model_width)
    d_mid, d_scale_two, d_shift_two = second_back(d_mlp_in)
    d_mid = d_mid + grad_top
    d_gamma_one = jnp.sum(d_mid * attn_branch, axis=1)
    d_attn = gamma_one[:, None] * d_mid
    d_proj_bias = jnp.sum(d_attn, axis=(0, 1))
    d_attn_low = d_attn.astype(jnp.bfloat16).reshape(row_count, model_width)
    g_proj = jnp.einsum("ri,rd->id", heads_out, d_attn_low, preferred_element_type=jnp.float32)
    d_heads = jnp.einsum("rd,id->ri", d_attn_low, full_proj, preferred_element_type=jnp.float32)
    d_heads = d_heads.astype(jnp.bfloat16).reshape(head_shape)
    d_heads_all = group_send(d_heads.reshape(group_shape))
    probs = probs_low.astype(jnp.float32)
    d_probs = jnp.einsum(
        "amqgd,bmkgd->mgaqbk", d_heads_all, values_all, preferred_element_type=jnp.float32
    )
    row_delta = jnp.sum(probs * d_probs, axis=(-2, -1), keepdims=True)
    d_scores = (probs * (d_probs - row_delta)).astype(jnp.bfloat16)
    probs_again = probs_low
    d_query_all = jnp.einsum(
        "mgaqbk,bmkgd->amqgd", d_scores, keys_all, preferred_element_type=jnp.float32
    ).astype(jnp.bfloat16)
    d_key_all = jnp.einsum(
        "mgaqbk,amqgd->bmkgd", d_scores, query_all, preferred_element_type=jnp.float32
    ).astype(jnp.bfloat16)
    d_value_all = jnp.einsum(
        "mgaqbk,amqgd->bmkgd", probs_again, d_heads_all, preferred_element_type=jnp.float32
    ).astype(jnp.bfloat16)
    d_query_unit = group_return(d_query_all).reshape(head_shape).astype(jnp.float32)
    d_key_unit = group_return(d_key_all).reshape(head_shape).astype(jnp.float32)
    d_value = group_return(d_value_all).reshape(head_shape).astype(jnp.float32)
    d_query, d_head_scale = query_back(d_query_unit)
    (d_key,) = key_back(d_key_unit)
    d_query = d_query.reshape(map_count, piece_rows, local_width)
    d_key = d_key.reshape(map_count, piece_rows, local_width)
    d_value = d_value.reshape(map_count, piece_rows, local_width)
    d_query_bias = jnp.sum(d_query, axis=(0, 1))
    d_value_bias = jnp.sum(d_value, axis=(0, 1))
    d_qkv = (
        jnp.stack([d_query, d_key, d_value], axis=2)
        .astype(jnp.bfloat16)
        .reshape(row_count, 3 * local_width)
    )
    g_qkv = jnp.einsum("rd,rc->dc", attn_in, d_qkv, preferred_element_type=jnp.float32).reshape(
        model_width, 3, local_width
    )
    d_attn_in_part = jnp.einsum("rc,dc->rd", d_qkv, qkv_matrix, preferred_element_type=jnp.float32)
    d_attn_in = tp_sum(d_attn_in_part).reshape(map_count, piece_rows, model_width)
    d_input, d_scale_one, d_shift_one = first_back(d_attn_in)
    d_input = d_input + d_mid
    d_mod_part = jnp.stack(
        [d_gamma_one, d_gamma_two, d_scale_one, d_scale_two, d_shift_one, d_shift_two], axis=1
    )
    d_mod = lax.psum(d_mod_part, "ctx").astype(jnp.bfloat16).reshape(map_count, 6 * model_width)
    d_mod_all = lax.all_gather(d_mod, "shard", axis=0, tiled=True)
    g_ada = jnp.einsum(
        "md,mc->dc", cond_cols, d_mod_all, preferred_element_type=jnp.float32
    ).reshape(ada_rows, 6, model_width)
    d_ada_bias = jnp.sum(d_mod_all.astype(jnp.float32), axis=0).reshape(6, model_width)
    d_cond_cols = jnp.einsum("mc,dc->md", d_mod_all, ada_local, preferred_element_type=jnp.float32)
    d_cond_in = lax.all_to_all(d_cond_cols, "shard", 0, 1, tiled=True)
    silu_value, silu_back = jax.vjp(jax.nn.silu, cond_wide)
    (d_cond,) = silu_back(d_cond_in)
    early_shards = (
        lax.psum_scatter(g_up.astype(jnp.bfloat16), "shard", scatter_dimension=0, tiled=True),
        lax.psum_scatter(g_proj.astype(jnp.bfloat16), "shard", scatter_dimension=1, tiled=True),
        lax.psum_scatter(g_down.astype(jnp.bfloat16), "shard", scatter_dimension=1, tiled=True),
    )
    early_summed = lax.psum(early_shards, "ctx")
    qkv_low, early_summed = lax.optimization_barrier((g_qkv.astype(jnp.bfloat16), early_summed))
    qkv_shard = lax.psum_scatter(qkv_low, "shard", scatter_dimension=0, tiled=True)
    qkv_summed = lax.psum(qkv_shard, "ctx")
    summed = tuple(
        (
            g.astype(jnp.float32)
            for g in (qkv_summed, early_summed[0], early_summed[1], early_summed[2])
        )
    )
    square_sums = jnp.stack(
        [jnp.sum(stream * stream), jnp.sum(attn_part * attn_part), jnp.sum(mlp_part * mlp_part)]
    )
    small_parts = (
        square_sums,
        d_query_bias,
        d_value_bias,
        d_head_scale,
        d_proj_bias,
        d_up_bias,
        d_down_bias,
    )
    small_flat = small_sum(jnp.concatenate(small_parts))
    small = []
    offset = 0
    for part in small_parts:
        small.append(small_flat[offset : offset + part.shape[0]])
        offset += part.shape[0]
    entry_total = map_count * map_length * model_width * lax.axis_size("shard")
    norm_stats = jnp.sqrt(small[0] / entry_total)
    return (
        stream.astype(jnp.bfloat16),
        d_input.astype(jnp.bfloat16),
        d_cond,
        g_ada,
        d_ada_bias,
        summed[0],
        small[1],
        small[2],
        small[3],
        summed[2],
        small[4],
        summed[1],
        small[5],
        summed[3],
        small[6],
        norm_stats,
    )


def solution(mesh):
    in_specs = (
        P("shard", "ctx", None),
        P("shard", None),
        P("shard", None),
        P("shard", None, None),
        P(),
        P("shard", None, "tp"),
        P("tp"),
        P("tp"),
        P("tp"),
        P("tp", "shard"),
        P(),
        P("shard", "tp"),
        P("tp"),
        P("tp", "shard"),
        P(),
        P("shard", "ctx", None),
    )
    out_specs = (
        P("shard", "ctx", None),
        P("shard", "ctx", None),
        P("shard", None),
        P("shard", None, None),
        P(),
        P("shard", None, "tp"),
        P("tp"),
        P("tp"),
        P("tp"),
        P("tp", "shard"),
        P(),
        P("shard", "tp"),
        P("tp"),
        P("tp", "shard"),
        P(),
        P(),
    )
    return jax.shard_map(body, mesh=mesh, in_specs=in_specs, out_specs=out_specs, check_vma=False)
```

profile of v0, /device:TPU:0, one launch (start us, length us, event | category | flops | bytes accessed | tf_op | source)
XLA Modules:
  0.0 849.8 jit_solution(5357631159717462529)
XLA Ops:
  9.6 15.1 %all-gather.1 = bf16[4,6,1024]{2,1,0:T(8,128)(2,1)S(1)} all-gather(bf16[1,6,1024]{2,1,0:T(8,128)(2,1)} %bitcast.391), channel_id=1, replica_groups=mesh['shard'=4,'ctx'=4,'tp'=2] {'shard'}, dimensions={0}, use_global_device_ids=true | all-gather | bytes 61440 | tf_op jit(solution)/shard_map/all_gather | solution.py:145
  29.9 33.7 %fusion = f32[8,6144]{1,0:T(8,128)S(1)} fusion(f32[24,6144]{1,0:T(8,128)} %fusion.65), kind=kCustom, calls=%all-reduce-scatter | all-reduce-scatter fusion | flops 196609 | bytes 786944
  63.6 4.5 collective-permute-start.34
  71.8 10.8 %pad_maximum_fusion = bf16[1179648]{0:T(1024)(128)(2,1)} fusion(bf16[524288]{0:T(1024)(128)(2,1)S(1)} %bitcast.361, bf16[524288]{0:T(1024)(128)(2,1)S(1)} %bitcast.360, bf16[131072]{0:T(1024)(128)(2,1)S(1)} %bitcast.371), kind=kLoop, calls=%fused_computation.87 | loop fusion | flops 7077888 | bytes 4718592 | tf_op jit(solution)/shard_map/concatenate | solution.py:130
  85.7 4.6 broadcast_compare_fusion
  97.5 6.4 fusion.27
  131.5 5.7 collective-permute-done.7
  139.6 4.9 collective-permute-done.5
  146.9 5.9 collective-permute-done.4
  153.9 17.3 %select_reduce_fusion = (f32[6,2,4,170]{3,2,1,0:T(4,128)S(1)}, f32[6,2,4,170,4,170]{3,5,4,2,1,0:T(8,128)}) fusion(pred[6,4,170,4,170]{2,4,3,1,0:T(8,128)(4,1)} %broadcast_compare_fusion, bf16[1,6,170,2,64]{2,4,0,3,1:T(8,128)(2,1)} %bitcast.37, bf16[1,6,170,2,64]{2,4,0,3,1:T(8,128)(2,1)} %bitcast.35, bf16[1,6,170,2,64]{2,4,0,3,1:T(8,128)(2,1)} %bitcast.33, ...), kind=kOutput, calls=%fused_computation.12 | convolution fusion | flops 729691648 | bytes 27091200 | tf_op jit(solution)/shard_map/amqgd,bmkgd->mgaqbk/dot_general | solution.py:184
  171.3 15.7 %fusion.3 = f32[6,2,4,170]{3,2,1,0:T(4,128)S(1)} fusion(f32[6,2,4,170,4,170]{3,5,4,2,1,0:T(8,128)} %get-tuple-element.186, f32[6,2,4,170]{3,2,1,0:T(4,128)S(1)} %get-tuple-element.185, pred[6,4,170,4,170]{2,4,3,1,0:T(8,128)(4,1)} %broadcast_compare_fusion), kind=kLoop, calls=%fused_computation.13 | loop fusion | flops 16638240 | bytes 25034880 | tf_op jit(solution)/shard_map/reduce_sum | solution.py:192
  187.0 6.7 copy-done
  193.7 12.2 %divide_convert_fusion = bf16[6,2,4,170,4,170]{3,5,4,2,1,0:T(8,128)(2,1)} fusion(f32[6,2,4,170,4,170]{3,5,4,2,1,0:T(8,128)S(1)} %copy-done, f32[6,2,4,170]{3,2,1,0:T(4,128)S(1)} %fusion.3, f32[6,2,4,170]{3,2,1,0:T(4,128)S(1)} %get-tuple-element.185, pred[6,4,170,4,170]{2,4,3,1,0:T(8,128)(4,1)} %broadcast_compare_fusion), kind=kLoop, calls=%fused_computation.10 | loop fusion | flops 22195200 | bytes 36132480 | tf_op jit(solution)/shard_map/convert_element_type | solution.py:194
  205.9 9.6 %fusion.35 = bf16[4,6,170,2,64]{2,4,0,3,1:T(8,128)(2,1)S(1)} fusion(bf16[6,2,4,170,4,170]{3,5,4,2,1,0:T(8,128)(2,1)} %divide_convert_fusion, bf16[1,6,170,2,64]{2,4,0,3,1:T(8,128)(2,1)} %bitcast.15, bf16[1,6,170,2,64]{2,4,0,3,1:T(8,128)(2,1)} %bitcast.13, bf16[1,6,170,2,64]{2,4,0,3,1:T(8,128)(2,1)} %bitcast.11, ...), kind=kOutput, calls=%fused_computation.107 | convolution fusion | flops 714946560 | bytes 13186560 | tf_op jit(solution)/shard_map/mgaqbk,bmkgd->amqgd/dot_general | solution.py:195
  224.7 4.1 mul.528
  228.8 5.3 collective-permute-done.11
  241.0 18.9 %all-gather.8.cloned.1.call-done = bf16[4718592]{0:T(1024)(128)(2,1)} async-done(((bf16[1179648]{0:T(1024)(128)(2,1)}), bf16[4718592]{0:T(1024)(128)(2,1)}) %all-gather.8.cloned.1.call-update) | async-done | bytes 9437200 | tf_op jit(solution)/shard_map/all_gather | solution.py:133
  259.9 12.5 %reshape.660 = bf16[4,1179648]{1,0:T(4,128)(2,1)} reshape(bf16[4718592]{0:T(1024)(128)(2,1)} %all-gather.8.cloned.1.call-done) | data formatting | bytes 18874368 | tf_op jit(solution)/shard_map/all_gather | solution.py:133
  278.0 8.3 fusion.72
  286.4 8.0 reshape_reshape.7
  294.4 4.8 copy.349
  299.2 6.4 copy.241
  305.6 9.2 %multiply_reduce_fusion.6 = (f32[]{:T(128)}, f32[1020,1024]{1,0:T(8,128)}) fusion(f32[1020,1024]{1,0:T(8,128)} %mul.528, f32[1024]{0:T(1024)S(1)} %copy-done.76, f32[1020,1024]{1,0:T(8,128)} %fusion.76, f32[1020,1024]{1,0:T(8,128)} %collective-permute-done.12), kind=kLoop, calls=%fused_computation.58 | loop fusion | flops 5222399 | bytes 16715780 | tf_op jit(solution)/shard_map/reduce_sum | solution.py:302
  314.8 4.3 reshape.590
  327.9 7.5 fusion.77
  335.5 10.6 %fusion.69 = (f32[2048]{0:T(1024)}, bf16[1020,2048]{1,0:T(8,128)(2,1)S(1)}) fusion(f32[1020,2048]{1,0:T(8,128)S(1)} %fusion.77, f32[2048]{0:T(1024)S(1)} %copy-done.97, bf16[1020,1024]{1,0:T(8,128)(2,1)S(1)} %copy-done.30, bf16[2048,1024]{0,1:T(8,128)(2,1)S(1)} %bitcast.356), kind=kOutput, calls=%fused_computation.244 | convolution fusion | flops 4324145152 | bytes 18833408 | tf_op jit(solution)/shard_map/rd,fd->rf/dot_general | solution.py:218
  346.2 6.1 fusion.32
  352.8 6.9 fusion.67
  362.2 4.1 mul.531
  366.4 6.8 add.447
  373.2 4.2 reshape.596
  377.4 9.3 %multiply_reduce_fusion.5 = (f32[]{:T(128)}, f32[1020,1024]{1,0:T(8,128)}) fusion(f32[1020,1024]{1,0:T(8,128)} %mul.531, f32[1024]{0:T(1024)S(1)} %copy-done.85, f32[1020,1024]{1,0:T(8,128)} %fusion.67, f32[1020,1024]{1,0:T(8,128)} %collective-permute-done.13), kind=kLoop, calls=%fused_computation.57 | loop fusion | flops 5222399 | bytes 16715780 | tf_op jit(solution)/shard_map/reduce_sum | solution.py:302
  386.7 4.3 reshape.594
  391.0 8.4 multiply_reduce_fusion
  399.4 3.5 multiply_reduce_fusion.1
  402.9 5.7 multiply_reduce_fusion.7
  413.2 4.0 convolution_convert_fusion.3
  417.2 8.3 convolution_convert_fusion.1
  442.7 11.9 %convolution_convert_fusion = bf16[2048,1024]{1,0:T(8,128)(2,1)} fusion(bf16[1020,1024]{1,0:T(8,128)(2,1)S(1)} %copy-done.31, f32[1020,2048]{1,0:T(8,128)} %copy-done.102, f32[2048]{0:T(1024)S(1)} %copy-done.98), kind=kOutput, calls=%fused_computation.65 | convolution fusion | flops 4301176832 | bytes 14647296 | tf_op jit(solution)/shard_map/rf,rd->fd/dot_general | solution.py:217
  460.0 11.7 %fusion.38 = bf16[4,6,170,2,64]{2,4,0,3,1:T(8,128)(2,1)S(1)} fusion(bf16[6,2,4,170,4,170]{3,5,4,2,1,0:T(8,128)(2,1)} %divide_convert_fusion, bf16[1,6,170,2,64]{2,4,0,3,1:T(8,128)(2,1)} %bitcast.369, bf16[1,6,170,2,64]{2,4,0,3,1:T(8,128)(2,1)S(1)} %bitcast.367, bf16[1,6,170,2,64]{2,4,0,3,1:T(8,128)(2,1)S(1)} %bitcast.365, ...), kind=kOutput, calls=%fused_computation.110 | convolution fusion | flops 714946560 | bytes 13186560 | tf_op jit(solution)/shard_map/mgaqbk,amqgd->bmkgd/dot_general | solution.py:248
  471.7 18.4 %fusion.1 = (f32[6,2,4,170]{3,2,1,0:T(4,128)S(1)}, f32[6,2,4,170,4,170]{3,5,4,2,1,0:T(8,128)}) fusion(bf16[6,2,4,170,4,170]{3,5,4,2,1,0:T(8,128)(2,1)} %divide_convert_fusion, bf16[1,6,170,2,64]{2,4,0,3,1:T(8,128)(2,1)} %bitcast.15, bf16[1,6,170,2,64]{2,4,0,3,1:T(8,128)(2,1)} %bitcast.13, bf16[1,6,170,2,64]{2,4,0,3,1:T(8,128)(2,1)} %bitcast.11, ...), kind=kOutput, calls=%fused_computation.8 | convolution fusion | flops 735240448 | bytes 35414400 | tf_op jit(solution)/shard_map/amqgd,bmkgd->mgaqbk/dot_general | solution.py:236
  494.6 23.8 %fusion.2 = bf16[6,2,4,170,4,170]{3,5,4,2,1,0:T(8,128)(2,1)S(1)} fusion(f32[6,2,4,170,4,170]{3,5,4,2,1,0:T(8,128)} %get-tuple-element.188, f32[6,2,4,170]{3,2,1,0:T(4,128)S(1)} %get-tuple-element.187, f32[6,2,4,170]{3,2,1,0:T(4,128)S(1)} %copy-done.55, f32[6,2,4,170]{3,2,1,0:T(4,128)S(1)} %copy-done.53, f32[6,2,4,170,4,170]{3,5,4,2,1,0:T(8,128)} %get-tuple-element.186, ...), kind=kLoop, calls=%fused_computation.9 | loop fusion | flops 44390400 | bytes 58360320 | tf_op jit(solution)/shard_map/convert_element_type | solution.py:240
  518.4 6.0 copy-done.1
  524.4 4.4 fusion.36
  528.8 12.4 %fusion.37 = bf16[4,6,170,2,64]{2,4,0,3,1:T(8,128)(2,1)S(1)} fusion(bf16[6,2,4,170,4,170]{3,5,4,2,1,0:T(8,128)(2,1)} %copy-done.1, bf16[1,6,170,2,64]{2,4,0,3,1:T(8,128)(2,1)} %bitcast.381, bf16[1,6,170,2,64]{2,4,0,3,1:T(8,128)(2,1)} %bitcast.383, bf16[1,6,170,2,64]{2,4,0,3,1:T(8,128)(2,1)} %bitcast.385, bf16[1,6,170,2,64]{2,4,0,3,1:T(8,128)(2,1)} %get-tuple-element.162), kind=kOutput, calls=%fused_computation.109 | convolution fusion | flops 714946560 | bytes 13186560 | tf_op jit(solution)/shard_map/mgaqbk,amqgd->bmkgd/dot_general | solution.py:245
  556.5 7.3 collective-permute-done.23
  571.8 7.2 collective-permute-done.20
  586.5 4.9 convert_bitcast_fusion.1
  620.8 3.5 copy.261
  631.4 3.5 copy.255
  634.9 9.1 %add_add_fusion.4 = (bf16[6,170,1,512]{3,1,2,0:T(8,128)(2,1)}, bf16[6,170,1,512]{3,1,2,0:T(8,128)(2,1)}) fusion(f32[6,170,1,512]{3,1,2,0:T(8,128)} %copy.255, f32[6,170,1,512]{3,1,2,0:T(8,128)} %copy.253, f32[6,170,1,512]{3,1,2,0:T(8,128)S(1)} %copy-done.18, f32[512]{0:T(512)S(1)} %copy-done.80, f32[512]{0:T(512)S(1)} %mul.494, ...), kind=kLoop, calls=%fused_computation.68 | loop fusion | flops 6266880 | bytes 18804736 | tf_op jit(solution)/shard_map/transpose(jvp())/add_any | solution.py:18
  654.5 7.0 fusion.78
  661.5 4.9 convolution_convert_fusion.2
  667.4 47.9 %all-reduce.9.cloned.1.call-done = (bf16[256,2048]{1,0:T(8,128)(2,1)}, bf16[512,256]{1,0:T(8,128)(2,1)}, bf16[2048,256]{1,0:T(8,128)(2,1)}) async-done(((bf16[256,2048]{1,0:T(8,128)(2,1)}, bf16[512,256]{1,0:T(8,128)(2,1)}, bf16[2048,256]{1,0:T(8,128)(2,1)}), (bf16[256,2048]{1,0:T(8,128)(2,1)}, bf16[512,256]{1,0:T(8,128)(2,1)}, bf16[2048,256]{1,0:T(8,128)(2,1)})) %all-reduce.9.cloned.1.call-update) | async-done | bytes 2359312 | tf_op jit(solution)/shard_map/psum | solution.py:291
  721.8 4.7 collective-permute-done.32
  730.6 6.9 add.451
  737.5 4.3 reshape.598
  741.9 3.5 fusion.68
  747.9 19.0 %all-reduce.10 = bf16[6,6,1024]{2,1,0:T(8,128)(2,1)S(1)} all-reduce(f32[6,6,1024]{2,1,0:T(8,128)S(1)} %stack.200), channel_id=1, replica_groups=mesh['shard'=4,'ctx'=4,'tp'=2] {'ctx'}, use_global_device_ids=true, to_apply=%region_24.26 | all-reduce | flops 36864 | bytes 221184 | tf_op jit(solution)/shard_map/psum | solution.py:276
  766.9 21.6 %all-gather.2 = bf16[4,6,6144]{2,1,0:T(8,128)(2,1)S(1)} all-gather(bf16[1,6,6144]{2,1,0:T(8,128)(2,1)S(1)} %reshape.667), channel_id=1, replica_groups=mesh['shard'=4,'ctx'=4,'tp'=2] {'shard'}, dimensions={0}, use_global_device_ids=true | all-gather | bytes 368640 | tf_op jit(solution)/shard_map/all_gather | solution.py:277
  788.5 5.3 add_convert_fusion
  800.4 4.4 fusion.66
  805.5 6.7 copy.279
  816.7 23.3 %all-reduce.7.cloned.1.call-done = bf16[256,3,512]{2,0,1:T(8,128)(2,1)} async-done(((bf16[256,3,512]{2,0,1:T(8,128)(2,1)}), bf16[256,3,512]{2,0,1:T(8,128)(2,1)}) %all-reduce.7.cloned.1.call-update) | async-done | bytes 786448 | tf_op jit(solution)/shard_map/psum | solution.py:294
  (461 shorter events, 224.8 us)
Async XLA Ops:
  7.2 90.3 %all-gather.6.cloned.1.call-start = ((), (), s32[]{:S(2)}) async-start(), calls=%async_computation.5 | async-start | bytes 3932160 | tf_op jit(solution)/shard_map/all_gather | solution.py:129
  9.5 250.4 %all-gather.8.cloned.1.call-start = ((), (), s32[]{:S(2)}) async-start(), calls=%async_computation.11 | async-start | bytes 11796480 | tf_op jit(solution)/shard_map/all_gather | solution.py:133
  28.0 42.7 %copy-start.11 = (bf16[256,6,1024]{0,2,1:T(8,128)(2,1)}, bf16[256,6,1024]{0,2,1:T(8,128)(2,1)S(1)}, u32[]{:S(2)}) copy-start(bf16[256,6,1024]{0,2,1:T(8,128)(2,1)S(1)} %copy.226) | copy-start | bytes 9437188
  63.6 29.0 %collective-permute-start.34 = (f32[6,6144]{1,0:T(8,128)S(1)}, f32[6,6144]{1,0:T(8,128)}, u32[]{:S(2)}, u32[]{:S(2)}) collective-permute-start(f32[6,6144]{1,0:T(8,128)S(1)} %slice.187), channel_id=1, source_target_pairs={{0,8},{8,16},{16,24},{1,9},{9,17},{17,25},{2,10},{10,18},{18,26},{... | collective-permute-start | bytes 442376
  71.8 11.9 %copy-start.3 = (bf16[6,170,1024]{2,1,0:T(8,128)(2,1)S(1)}, bf16[6,170,1024]{2,1,0:T(8,128)(2,1)}, u32[]{:S(2)}) copy-start(bf16[6,170,1024]{2,1,0:T(8,128)(2,1)} %param.18) | copy-start | bytes 6266884
  82.7 561.3 %reduce-scatter.9.cloned.1.call-start = ((), (), s32[]{:S(2)}) async-start(), calls=%async_computation.7 | async-start | bytes 1310720 | tf_op jit(solution)/shard_map/reduce_scatter | solution.py:288
  90.5 32.7 %copy-start.72 = (f32[4,2,64]{2,1,0:T(2,128)}, f32[4,2,64]{2,1,0:T(2,128)S(1)}, u32[]{:S(2)}) copy-start(f32[4,2,64]{2,1,0:T(2,128)S(1)} %add.420) | copy-start | bytes 6148
  90.5 30.9 %copy-start.74 = (f32[8,64]{1,0:T(8,128)}, f32[8,64]{1,0:T(8,128)S(1)}, u32[]{:S(2)}) copy-start(f32[8,64]{1,0:T(8,128)S(1)} %add.423) | copy-start | bytes 6148
  90.6 32.5 %copy-start.81 = (f32[4,2]{1,0:T(4,128)}, f32[4,2]{1,0:T(4,128)S(1)}, u32[]{:S(2)}) copy-start(f32[4,2]{1,0:T(4,128)S(1)} %mul.452) | copy-start | bytes 100
  115.4 13.1 %collective-permute-start.8 = (bf16[6,170,2,64]{1,3,2,0:T(8,128)(2,1)}, bf16[6,170,2,64]{1,3,2,0:T(8,128)(2,1)}, u32[]{:S(2)}, u32[]{:S(2)}) collective-permute-start(bf16[6,170,2,64]{1,3,2,0:T(8,128)(2,1)} %get-tuple-element.167), channel_id=1, source_target_pairs={{0,6},{2,0},{4,2},{6,4},{1,7},{3,1},{5,3},{7,5},{8,14},{10,8},{12,... | collective-permute-start | bytes 783368 | tf_op jit(solution)/shard_map/ppermute | solution.py:63
  117.8 19.5 %collective-permute-start.7 = (bf16[6,170,2,64]{1,3,2,0:T(8,128)(2,1)}, bf16[6,170,2,64]{1,3,2,0:T(8,128)(2,1)}, u32[]{:S(2)}, u32[]{:S(2)}) collective-permute-start(bf16[6,170,2,64]{1,3,2,0:T(8,128)(2,1)} %get-tuple-element.168), channel_id=1, source_target_pairs={{0,4},{2,6},{4,0},{6,2},{1,5},{3,7},{5,1},{7,3},{8,12},{10,14},{12... | collective-permute-start | bytes 783368 | tf_op jit(solution)/shard_map/ppermute | solution.py:63
  118.3 20.8 %collective-permute-start.6 = (bf16[6,170,2,64]{1,3,2,0:T(8,128)(2,1)}, bf16[6,170,2,64]{1,3,2,0:T(8,128)(2,1)}, u32[]{:S(2)}, u32[]{:S(2)}) collective-permute-start(bf16[6,170,2,64]{1,3,2,0:T(8,128)(2,1)} %get-tuple-element.169), channel_id=1, source_target_pairs={{0,2},{2,4},{4,6},{6,0},{1,3},{3,5},{5,7},{7,1},{8,10},{10,12},{12... | collective-permute-start | bytes 783368 | tf_op jit(solution)/shard_map/ppermute | solution.py:63
  124.6 19.9 %collective-permute-start.5 = (bf16[6,170,2,64]{1,3,2,0:T(8,128)(2,1)S(1)}, bf16[6,170,2,64]{1,3,2,0:T(8,128)(2,1)S(1)}, u32[]{:S(2)}, u32[]{:S(2)}) collective-permute-start(bf16[6,170,2,64]{1,3,2,0:T(8,128)(2,1)S(1)} %get-tuple-element.163), channel_id=1, source_target_pairs={{0,6},{2,0},{4,2},{6,4},{1,7},{3,1},{5,3},{7,5},{8,14},{10,8},{12,... | collective-permute-start | bytes 783368 | tf_op jit(solution)/shard_map/ppermute | solution.py:63
  126.9 25.8 %collective-permute-start.4 = (bf16[6,170,2,64]{1,3,2,0:T(8,128)(2,1)S(1)}, bf16[6,170,2,64]{1,3,2,0:T(8,128)(2,1)S(1)}, u32[]{:S(2)}, u32[]{:S(2)}) collective-permute-start(bf16[6,170,2,64]{1,3,2,0:T(8,128)(2,1)S(1)} %get-tuple-element.164), channel_id=1, source_target_pairs={{0,4},{2,6},{4,0},{6,2},{1,5},{3,7},{5,1},{7,3},{8,12},{10,14},{12... | collective-permute-start | bytes 783368 | tf_op jit(solution)/shard_map/ppermute | solution.py:63
  128.5 25.5 %collective-permute-start.3 = (bf16[6,170,2,64]{1,3,2,0:T(8,128)(2,1)S(1)}, bf16[6,170,2,64]{1,3,2,0:T(8,128)(2,1)S(1)}, u32[]{:S(2)}, u32[]{:S(2)}) collective-permute-start(bf16[6,170,2,64]{1,3,2,0:T(8,128)(2,1)S(1)} %get-tuple-element.165), channel_id=1, source_target_pairs={{0,2},{2,4},{4,6},{6,0},{1,3},{3,5},{5,7},{7,1},{8,10},{10,12},{12... | collective-permute-start | bytes 783368 | tf_op jit(solution)/shard_map/ppermute | solution.py:63
  130.1 23.8 %copy-start.35 = (bf16[1,6,170,2,64]{2,4,0,3,1:T(8,128)(2,1)S(1)}, bf16[1,6,170,2,64]{2,4,0,3,1:T(8,128)(2,1)}, u32[]{:S(2)}) copy-start(bf16[1,6,170,2,64]{2,4,0,3,1:T(8,128)(2,1)} %get-tuple-element.166) | copy-start | bytes 783364
  130.1 23.8 %copy-start.37 = (bf16[1,6,170,2,64]{2,4,0,3,1:T(8,128)(2,1)S(1)}, bf16[1,6,170,2,64]{2,4,0,3,1:T(8,128)(2,1)}, u32[]{:S(2)}) copy-start(bf16[1,6,170,2,64]{2,4,0,3,1:T(8,128)(2,1)} %get-tuple-element.162) | copy-start | bytes 783364
  131.5 74.4 %copy-start.26 = (bf16[1,6,170,2,64]{2,4,0,3,1:T(8,128)(2,1)}, bf16[1,6,170,2,64]{2,4,0,3,1:T(8,128)(2,1)S(1)}, u32[]{:S(2)}) copy-start(bf16[1,6,170,2,64]{2,4,0,3,1:T(8,128)(2,1)S(1)} %get-tuple-element.158) | copy-start | bytes 783364
  137.2 68.7 %collective-permute-start.2 = (bf16[6,170,2,64]{1,3,2,0:T(8,128)(2,1)}, bf16[6,170,2,64]{1,3,2,0:T(8,128)(2,1)}, u32[]{:S(2)}, u32[]{:S(2)}) collective-permute-start(bf16[6,170,2,64]{1,3,2,0:T(8,128)(2,1)} %get-tuple-element.159), channel_id=1, source_target_pairs={{0,6},{2,0},{4,2},{6,4},{1,7},{3,1},{5,3},{7,5},{8,14},{10,8},{12,... | collective-permute-start | bytes 783368 | tf_op jit(solution)/shard_map/ppermute | solution.py:63
  139.1 66.9 %collective-permute-start.1 = (bf16[6,170,2,64]{1,3,2,0:T(8,128)(2,1)}, bf16[6,170,2,64]{1,3,2,0:T(8,128)(2,1)}, u32[]{:S(2)}, u32[]{:S(2)}) collective-permute-start(bf16[6,170,2,64]{1,3,2,0:T(8,128)(2,1)} %get-tuple-element.160), channel_id=1, source_target_pairs={{0,4},{2,6},{4,0},{6,2},{1,5},{3,7},{5,1},{7,3},{8,12},{10,14},{12... | collective-permute-start | bytes 783368 | tf_op jit(solution)/shard_map/ppermute | solution.py:63
  144.5 26.8 %copy-start.56 = (bf16[6,170,2,64]{1,3,2,0:T(8,128)(2,1)}, bf16[6,170,2,64]{1,3,2,0:T(8,128)(2,1)S(1)}, u32[]{:S(2)}) copy-start(bf16[6,170,2,64]{1,3,2,0:T(8,128)(2,1)S(1)} %collective-permute-done.5) | copy-start | bytes 783364
  144.5 61.5 %collective-permute-start = (bf16[6,170,2,64]{1,3,2,0:T(8,128)(2,1)}, bf16[6,170,2,64]{1,3,2,0:T(8,128)(2,1)}, u32[]{:S(2)}, u32[]{:S(2)}) collective-permute-start(bf16[6,170,2,64]{1,3,2,0:T(8,128)(2,1)} %get-tuple-element.161), channel_id=1, source_target_pairs={{0,2},{2,4},{4,6},{6,0},{1,3},{3,5},{5,7},{7,1},{8,10},{10,12},{12... | collective-permute-start | bytes 783368 | tf_op jit(solution)/shard_map/ppermute | solution.py:63
  152.8 18.5 %copy-start.57 = (bf16[6,170,2,64]{1,3,2,0:T(8,128)(2,1)}, bf16[6,170,2,64]{1,3,2,0:T(8,128)(2,1)S(1)}, u32[]{:S(2)}) copy-start(bf16[6,170,2,64]{1,3,2,0:T(8,128)(2,1)S(1)} %collective-permute-done.4) | copy-start | bytes 783364
  153.9 17.3 %copy-start.58 = (bf16[6,170,2,64]{1,3,2,0:T(8,128)(2,1)}, bf16[6,170,2,64]{1,3,2,0:T(8,128)(2,1)S(1)}, u32[]{:S(2)}) copy-start(bf16[6,170,2,64]{1,3,2,0:T(8,128)(2,1)S(1)} %collective-permute-done.3) | copy-start | bytes 783364
  171.3 15.8 %copy-start.52 = (f32[6,2,4,170]{3,2,1,0:T(4,128)}, f32[6,2,4,170]{3,2,1,0:T(4,128)S(1)}, u32[]{:S(2)}) copy-start(f32[6,2,4,170]{3,2,1,0:T(4,128)S(1)} %get-tuple-element.185) | copy-start | bytes 97924
  171.3 22.4 %copy-start = (f32[6,2,4,170,4,170]{3,5,4,2,1,0:T(8,128)S(1)}, f32[6,2,4,170,4,170]{3,5,4,2,1,0:T(8,128)}, u32[]{:S(2)}) copy-start(f32[6,2,4,170,4,170]{3,5,4,2,1,0:T(8,128)} %get-tuple-element.186) | copy-start | bytes 66585604
  193.7 12.2 %copy-start.54 = (f32[6,2,4,170]{3,2,1,0:T(4,128)}, f32[6,2,4,170]{3,2,1,0:T(4,128)S(1)}, u32[]{:S(2)}) copy-start(f32[6,2,4,170]{3,2,1,0:T(4,128)S(1)} %fusion.3) | copy-start | bytes 97924
  216.6 12.3 %collective-permute-start.9 = (bf16[6,170,2,64]{1,3,2,0:T(8,128)(2,1)}, bf16[6,170,2,64]{1,3,2,0:T(8,128)(2,1)S(1)}, u32[]{:S(2)}, u32[]{:S(2)}) collective-permute-start(bf16[6,170,2,64]{1,3,2,0:T(8,128)(2,1)} %get-tuple-element.155), channel_id=1, source_target_pairs={{0,6},{2,0},{4,2},{6,4},{1,7},{3,1},{5,3},{7,5},{8,14},{10,8},{12,... | collective-permute-start | bytes 783368 | tf_op jit(solution)/shard_map/ppermute | solution.py:74
  218.6 15.5 %collective-permute-start.11 = (bf16[6,170,2,64]{1,3,2,0:T(8,128)(2,1)}, bf16[6,170,2,64]{1,3,2,0:T(8,128)(2,1)}, u32[]{:S(2)}, u32[]{:S(2)}) collective-permute-start(bf16[6,170,2,64]{1,3,2,0:T(8,128)(2,1)} %get-tuple-element.156), channel_id=1, source_target_pairs={{0,2},{2,4},{4,6},{6,0},{1,3},{3,5},{5,7},{7,1},{8,10},{10,12},{12... | collective-permute-start | bytes 783368 | tf_op jit(solution)/shard_map/ppermute | solution.py:74
  218.7 16.8 %collective-permute-start.10 = (bf16[6,170,2,64]{1,3,2,0:T(8,128)(2,1)S(1)}, bf16[6,170,2,64]{1,3,2,0:T(8,128)(2,1)}, u32[]{:S(2)}, u32[]{:S(2)}) collective-permute-start(bf16[6,170,2,64]{1,3,2,0:T(8,128)(2,1)S(1)} %get-tuple-element.157), channel_id=1, source_target_pairs={{0,4},{2,6},{4,0},{6,2},{1,5},{3,7},{5,1},{7,3},{8,12},{10,14},{12... | collective-permute-start | bytes 783368 | tf_op jit(solution)/shard_map/ppermute | solution.py:74
  278.0 27.5 %collective-permute-start.12 = (f32[1020,1024]{1,0:T(8,128)}, f32[1020,1024]{1,0:T(8,128)}, u32[]{:S(2)}, u32[]{:S(2)}) collective-permute-start(f32[1020,1024]{1,0:T(8,128)} %fusion.76), channel_id=1, source_target_pairs={{0,1},{1,0},{2,3},{3,2},{4,5},{5,4},{6,7},{7,6},{8,9},{9,8},{10,11... | collective-permute-start | bytes 12533768 | tf_op jit(solution)/shard_map/ppermute | solution.py:34
  335.5 17.3 %copy-start.102 = (f32[1020,2048]{1,0:T(8,128)}, f32[1020,2048]{1,0:T(8,128)S(1)}, u32[]{:S(2)}) copy-start(f32[1020,2048]{1,0:T(8,128)S(1)} %fusion.77) | copy-start | bytes 25067524
  352.3 14.1 %collective-permute-start.14 = (f32[1020,1024]{1,0:T(8,128)}, f32[1020,1024]{1,0:T(8,128)}, u32[]{:S(2)}, u32[]{:S(2)}) collective-permute-start(f32[1020,1024]{1,0:T(8,128)} %fusion.32), channel_id=1, source_target_pairs={{0,1},{1,0},{2,3},{3,2},{4,5},{5,4},{6,7},{7,6},{8,9},{9,8},{10,11... | collective-permute-start | bytes 12533768 | tf_op jit(solution)/shard_map/ppermute | solution.py:34
  359.7 17.7 %collective-permute-start.13 = (f32[1020,1024]{1,0:T(8,128)}, f32[1020,1024]{1,0:T(8,128)}, u32[]{:S(2)}, u32[]{:S(2)}) collective-permute-start(f32[1020,1024]{1,0:T(8,128)} %fusion.67), channel_id=1, source_target_pairs={{0,1},{1,0},{2,3},{3,2},{4,5},{5,4},{6,7},{7,6},{8,9},{9,8},{10,11... | collective-permute-start | bytes 12533768 | tf_op jit(solution)/shard_map/ppermute | solution.py:34
  386.7 12.7 %slice-start = ((s8[4325376]{0:T(1024)(128)(4,1)}), s8[131072]{0:T(1024)(128)(4,1)S(1)}, s32[]{:S(2)}) async-start(s8[4325376]{0:T(1024)(128)(4,1)} %bitcast.328), calls=%async_computation.13 | async-start | bytes 262144
  417.2 226.8 %reduce-scatter.7.cloned.1.call-start = ((), (), s32[]{:S(2)}) async-start(), calls=%async_computation.6 | async-start | bytes 5242880 | tf_op jit(solution)/shard_map/reduce_scatter | solution.py:287
  425.6 218.4 %reduce-scatter.11.cloned.1.call-start = ((), (), s32[]{:S(2)}) async-start(), calls=%async_computation.8 | async-start | bytes 5242880 | tf_op jit(solution)/shard_map/reduce_scatter | solution.py:289
  438.3 18.9 %collective-permute-start.15 = (bf16[6,170,2,64]{1,3,2,0:T(8,128)(2,1)S(1)}, bf16[6,170,2,64]{1,3,2,0:T(8,128)(2,1)S(1)}, u32[]{:S(2)}, u32[]{:S(2)}) collective-permute-start(bf16[6,170,2,64]{1,3,2,0:T(8,128)(2,1)S(1)} %bitcast.378), channel_id=1, source_target_pairs={{0,2},{2,4},{4,6},{6,0},{1,3},{3,5},{5,7},{7,1},{8,10},{10,12},{12... | collective-permute-start | bytes 783368 | tf_op jit(solution)/shard_map/ppermute | solution.py:63
  439.8 19.4 %collective-permute-start.16 = (bf16[6,170,2,64]{1,3,2,0:T(8,128)(2,1)S(1)}, bf16[6,170,2,64]{1,3,2,0:T(8,128)(2,1)S(1)}, u32[]{:S(2)}, u32[]{:S(2)}) collective-permute-start(bf16[6,170,2,64]{1,3,2,0:T(8,128)(2,1)S(1)} %bitcast.377), channel_id=1, source_target_pairs={{0,4},{2,6},{4,0},{6,2},{1,5},{3,7},{5,1},{7,3},{8,12},{10,14},{12... | collective-permute-start | bytes 783368 | tf_op jit(solution)/shard_map/ppermute | solution.py:63
  441.3 18.0 %collective-permute-start.17 = (bf16[6,170,2,64]{1,3,2,0:T(8,128)(2,1)S(1)}, bf16[6,170,2,64]{1,3,2,0:T(8,128)(2,1)S(1)}, u32[]{:S(2)}, u32[]{:S(2)}) collective-permute-start(bf16[6,170,2,64]{1,3,2,0:T(8,128)(2,1)S(1)} %bitcast.376), channel_id=1, source_target_pairs={{0,6},{2,0},{4,2},{6,4},{1,7},{3,1},{5,3},{7,5},{8,14},{10,8},{12,... | collective-permute-start | bytes 783368 | tf_op jit(solution)/shard_map/ppermute | solution.py:63
  454.6 260.7 %all-reduce.9.cloned.1.call-start = ((), (), s32[]{:S(2)}) async-start(), calls=%async_computation.12 | async-start | bytes 4718592 | tf_op jit(solution)/shard_map/psum | solution.py:291
  491.2 55.1 %collective-permute-start.24 = (bf16[6,170,2,64]{1,3,2,0:T(8,128)(2,1)}, bf16[6,170,2,64]{1,3,2,0:T(8,128)(2,1)}, u32[]{:S(2)}, u32[]{:S(2)}) collective-permute-start(bf16[6,170,2,64]{1,3,2,0:T(8,128)(2,1)} %get-tuple-element.151), channel_id=1, source_target_pairs={{0,6},{2,0},{4,2},{6,4},{1,7},{3,1},{5,3},{7,5},{8,14},{10,8},{12,... | collective-permute-start | bytes 783368 | tf_op jit(solution)/shard_map/ppermute | solution.py:74
  492.8 54.0 %collective-permute-start.26 = (bf16[6,170,2,64]{1,3,2,0:T(8,128)(2,1)}, bf16[6,170,2,64]{1,3,2,0:T(8,128)(2,1)}, u32[]{:S(2)}, u32[]{:S(2)}) collective-permute-start(bf16[6,170,2,64]{1,3,2,0:T(8,128)(2,1)} %get-tuple-element.152), channel_id=1, source_target_pairs={{0,2},{2,4},{4,6},{6,0},{1,3},{3,5},{5,7},{7,1},{8,10},{10,12},{12... | collective-permute-start | bytes 783368 | tf_op jit(solution)/shard_map/ppermute | solution.py:74
  493.2 56.5 %collective-permute-start.25 = (bf16[6,170,2,64]{1,3,2,0:T(8,128)(2,1)}, bf16[6,170,2,64]{1,3,2,0:T(8,128)(2,1)}, u32[]{:S(2)}, u32[]{:S(2)}) collective-permute-start(bf16[6,170,2,64]{1,3,2,0:T(8,128)(2,1)} %get-tuple-element.153), channel_id=1, source_target_pairs={{0,4},{2,6},{4,0},{6,2},{1,5},{3,7},{5,1},{7,3},{8,12},{10,14},{12... | collective-permute-start | bytes 783368 | tf_op jit(solution)/shard_map/ppermute | solution.py:74
  494.6 29.8 %copy-start.36 = (bf16[1,6,170,2,64]{2,4,0,3,1:T(8,128)(2,1)S(1)}, bf16[1,6,170,2,64]{2,4,0,3,1:T(8,128)(2,1)}, u32[]{:S(2)}) copy-start(bf16[1,6,170,2,64]{2,4,0,3,1:T(8,128)(2,1)} %get-tuple-element.166) | copy-start | bytes 783364
  542.3 12.6 %collective-permute-start.21 = (bf16[6,170,2,64]{1,3,2,0:T(8,128)(2,1)}, bf16[6,170,2,64]{1,3,2,0:T(8,128)(2,1)}, u32[]{:S(2)}, u32[]{:S(2)}) collective-permute-start(bf16[6,170,2,64]{1,3,2,0:T(8,128)(2,1)} %get-tuple-element.147), channel_id=1, source_target_pairs={{0,6},{2,0},{4,2},{6,4},{1,7},{3,1},{5,3},{7,5},{8,14},{10,8},{12,... | collective-permute-start | bytes 783368 | tf_op jit(solution)/shard_map/ppermute | solution.py:74
  546.2 17.6 %collective-permute-start.23 = (bf16[6,170,2,64]{1,3,2,0:T(8,128)(2,1)}, bf16[6,170,2,64]{1,3,2,0:T(8,128)(2,1)}, u32[]{:S(2)}, u32[]{:S(2)}) collective-permute-start(bf16[6,170,2,64]{1,3,2,0:T(8,128)(2,1)} %get-tuple-element.148), channel_id=1, source_target_pairs={{0,2},{2,4},{4,6},{6,0},{1,3},{3,5},{5,7},{7,1},{8,10},{10,12},{12... | collective-permute-start | bytes 783368 | tf_op jit(solution)/shard_map/ppermute | solution.py:74
  546.2 20.8 %collective-permute-start.22 = (bf16[6,170,2,64]{1,3,2,0:T(8,128)(2,1)}, bf16[6,170,2,64]{1,3,2,0:T(8,128)(2,1)}, u32[]{:S(2)}, u32[]{:S(2)}) collective-permute-start(bf16[6,170,2,64]{1,3,2,0:T(8,128)(2,1)} %get-tuple-element.149), channel_id=1, source_target_pairs={{0,4},{2,6},{4,0},{6,2},{1,5},{3,7},{5,1},{7,3},{8,12},{10,14},{12... | collective-permute-start | bytes 783368 | tf_op jit(solution)/shard_map/ppermute | solution.py:74
  546.8 25.0 %collective-permute-start.18 = (bf16[6,170,2,64]{1,3,2,0:T(8,128)(2,1)}, bf16[6,170,2,64]{1,3,2,0:T(8,128)(2,1)}, u32[]{:S(2)}, u32[]{:S(2)}) collective-permute-start(bf16[6,170,2,64]{1,3,2,0:T(8,128)(2,1)} %get-tuple-element.143), channel_id=1, source_target_pairs={{0,6},{2,0},{4,2},{6,4},{1,7},{3,1},{5,3},{7,5},{8,14},{10,8},{12,... | collective-permute-start | bytes 783368 | tf_op jit(solution)/shard_map/ppermute | solution.py:74
  549.7 29.3 %collective-permute-start.20 = (bf16[6,170,2,64]{1,3,2,0:T(8,128)(2,1)}, bf16[6,170,2,64]{1,3,2,0:T(8,128)(2,1)}, u32[]{:S(2)}, u32[]{:S(2)}) collective-permute-start(bf16[6,170,2,64]{1,3,2,0:T(8,128)(2,1)} %get-tuple-element.144), channel_id=1, source_target_pairs={{0,2},{2,4},{4,6},{6,0},{1,3},{3,5},{5,7},{7,1},{8,10},{10,12},{12... | collective-permute-start | bytes 783368 | tf_op jit(solution)/shard_map/ppermute | solution.py:74
  554.9 26.6 %collective-permute-start.19 = (bf16[6,170,2,64]{1,3,2,0:T(8,128)(2,1)}, bf16[6,170,2,64]{1,3,2,0:T(8,128)(2,1)}, u32[]{:S(2)}, u32[]{:S(2)}) collective-permute-start(bf16[6,170,2,64]{1,3,2,0:T(8,128)(2,1)} %get-tuple-element.145), channel_id=1, source_target_pairs={{0,4},{2,6},{4,0},{6,2},{1,5},{3,7},{5,1},{7,3},{8,12},{10,14},{12... | collective-permute-start | bytes 783368 | tf_op jit(solution)/shard_map/ppermute | solution.py:74
  567.0 14.5 %copy-start.34 = (bf16[1,6,170,2,64]{2,4,3,1,0:T(8,128)(2,1)S(1)}, bf16[1,6,170,2,64]{2,4,3,1,0:T(8,128)(2,1)}, u32[]{:S(2)}) copy-start(bf16[1,6,170,2,64]{2,4,3,1,0:T(8,128)(2,1)} %get-tuple-element.142) | copy-start | bytes 783364
  610.9 55.6 %collective-permute-start.30 = (f32[5131]{0:T(1024)S(1)}, f32[5131]{0:T(1024)S(1)}, u32[]{:S(2)}, u32[]{:S(2)}) collective-permute-start(f32[5131]{0:T(1024)S(1)} %concatenate.7), channel_id=1, source_target_pairs={{0,6},{2,0},{4,2},{6,4},{1,7},{3,1},{5,3},{7,5},{8,14},{10,8},{12,... | collective-permute-start | bytes 61580 | tf_op jit(solution)/shard_map/ppermute | solution.py:86
  611.0 55.5 %collective-permute-start.29 = (f32[5131]{0:T(1024)S(1)}, f32[5131]{0:T(1024)S(1)}, u32[]{:S(2)}, u32[]{:S(2)}) collective-permute-start(f32[5131]{0:T(1024)S(1)} %concatenate.7), channel_id=1, source_target_pairs={{0,4},{2,6},{4,0},{6,2},{1,5},{3,7},{5,1},{7,3},{8,12},{10,14},{12... | collective-permute-start | bytes 61580 | tf_op jit(solution)/shard_map/ppermute | solution.py:86
  611.6 54.9 %collective-permute-start.28 = (f32[5131]{0:T(1024)S(1)}, f32[5131]{0:T(1024)S(1)}, u32[]{:S(2)}, u32[]{:S(2)}) collective-permute-start(f32[5131]{0:T(1024)S(1)} %concatenate.7), channel_id=1, source_target_pairs={{0,2},{2,4},{4,6},{6,0},{1,3},{3,5},{5,7},{7,1},{8,10},{10,12},{12... | collective-permute-start | bytes 61580 | tf_op jit(solution)/shard_map/ppermute | solution.py:86
  644.0 149.8 %reduce-scatter.13.cloned.1.call-start = ((), (), s32[]{:S(2)}) async-start(), calls=%async_computation.9 | async-start | bytes 3932160 | tf_op jit(solution)/shard_map/reduce_scatter | solution.py:293
  661.5 69.1 %collective-permute-start.27 = (f32[1020,1024]{1,0:T(8,128)}, f32[1020,1024]{1,0:T(8,128)}, u32[]{:S(2)}, u32[]{:S(2)}) collective-permute-start(f32[1020,1024]{1,0:T(8,128)} %fusion.78), channel_id=1, source_target_pairs={{0,1},{1,0},{2,3},{3,2},{4,5},{5,4},{6,7},{7,6},{8,9},{9,8},{10,11... | collective-permute-start | bytes 12533768 | tf_op jit(solution)/shard_map/ppermute | solution.py:34
  666.5 48.9 %copy-start.93 = (pred[4]{0:T(512)(128)(4,1)S(1)}, pred[4]{0:T(512)(128)(4,1)}, u32[]{:S(2)}) copy-start(pred[4]{0:T(512)(128)(4,1)} %get-tuple-element.190) | copy-start | bytes 16
  666.5 60.8 %copy-start.95 = (pred[4]{0:T(512)(128)(4,1)S(1)}, pred[4]{0:T(512)(128)(4,1)}, u32[]{:S(2)}) copy-start(pred[4]{0:T(512)(128)(4,1)} %compare_and_fusion.2) | copy-start | bytes 16
  715.4 124.6 %all-reduce.7.cloned.1.call-start = ((), (), s32[]{:S(2)}) async-start(), calls=%async_computation.10 | async-start | bytes 1572864 | tf_op jit(solution)/shard_map/psum | solution.py:294
  715.5 6.3 collective-permute-start.33
  718.9 7.6 collective-permute-start.32
  718.9 7.6 collective-permute-start.31
  797.1 15.1 %all-to-all-start = ((f32[4,6,256]{2,1,0:T(8,128)}), f32[4,6,256]{2,1,0:T(8,128)S(1)}, u32[]{:S(2)}, u32[]{:S(2)}) async-start(f32[4,6,256]{2,1,0:T(8,128)} %fusion.79), calls=%async_computation | async-start | bytes 65536 | tf_op jit(solution)/shard_map/all_to_all | solution.py:283
  (85 other events, 388.4 us)
Sparse Core Ops, SparseCore 0:
  10.1 78.9 all-gather.5
  90.7 169.1 all-gather.7
  417.3 25.5 reduce-scatter.8
  445.1 75.2 reduce-scatter.6
  522.5 77.3 reduce-scatter.10
  644.1 71.1 all-reduce.8
  717.6 64.7 reduce-scatter.12
  794.0 45.9 all-reduce.6
where the time goes:
time: 858 us; the launch traced here: 850 us
  local copies, waits for them, and re-layouts  199 us (23%)
  other arithmetic  185 us (22%)
  matrix products  163 us (19%)
  waiting for transfers between devices  147 us (17%)
  blocking collectives  89.4 us (10%)
  starting transfers between devices  49 us (6%)
  between operations  17 us (2%)
    unnamed x233, local copies, waits for them, and re-layouts  53.9 us
    psum x1, waiting for transfers between devices, body(): early_summed = lax.psum(early_shards, 'ctx')  47.9 us
    unnamed x1, blocking collectives  33.7 us
    ppermute x12, waiting for transfers between devices, group_return(): back.append(lax.ppermute(parts[shift], 'ctx', pairs))  30.5 us
    convert_element_type x1, other arithmetic, body(): d_scores = (probs * (d_probs - row_delta)).astype(jnp.bfloat16)  23.8 us
    psum x1, waiting for transfers between devices, body(): qkv_summed = lax.psum(qkv_shard, 'ctx')  23.3 us
    all_gather x1, blocking collectives, body(): d_mod_all = lax.all_gather(d_mod, 'shard', axis=0, tiled=True)  21.6 us
    ppermute x12, waiting for transfers between devices, group_send(): block = lax.ppermute(block, 'ctx', pairs)  19.6 us
  transfers between devices with their start and end apart: 44, of which 18 were waited for; matrix products, arithmetic and copies ran while one was open for 53% of the time, Pallas kernels for 0%

commit v1 on v0

--- a/solution.py
+++ b/solution.py
@@ -274,7 +274,16 @@
         [d_gamma_one, d_gamma_two, d_scale_one, d_scale_two, d_shift_one, d_shift_two], axis=1
     )
     d_mod = lax.psum(d_mod_part, "ctx").astype(jnp.bfloat16).reshape(map_count, 6 * model_width)
-    d_mod_all = lax.all_gather(d_mod, "shard", axis=0, tiled=True)
+    shard = d_mod
+    ways, here, lap = (lax.axis_size("shard"), lax.axis_index("shard"), shard.shape[0])
+    lengths = [n * ways if d == 0 else n for d, n in enumerate(shard.shape)]
+    full = lax.dynamic_update_slice_in_dim(
+        jnp.zeros(lengths, shard.dtype), shard, here * lap, axis=0
+    )
+    for far in range(1, ways):
+        shard = lax.ppermute(shard, "shard", [(d, (d + 1) % ways) for d in range(ways)])
+        full = lax.dynamic_update_slice_in_dim(full, shard, (here - far) % ways * lap, axis=0)
+    d_mod_all = full
     g_ada = jnp.einsum(
         "md,mc->dc", cond_cols, d_mod_all, preferred_element_type=jnp.float32
     ).reshape(ada_rows, 6, model_width)

time: 858 us -> 860 us (level)
  blocking collectives: 89.4 us -> 67.6 us
  starting transfers between devices: 49 us -> 61.4 us
    all_gather x1 -> x0, blocking collectives: 21.6 us -> none  [body(): d_mod_all = lax.all_gather(d_mod, 'shard', axis=0, tiled=True)]
    ppermute x0 -> x3, starting transfers between devices: none -> 11.8 us  [body(): lax.ppermute(shard, 'shard', [(d, (d + 1) % ways) for d in range(ways)])]
    unnamed x233 -> x232, local copies, waits for them, and re-layouts: 53.9 us -> 53.7 us
  transfers between devices with their start and end apart: 44 -> 47, of which waited for: 18 -> 21; matrix products, arithmetic and copies ran while one was open for 53% -> 53% of each run, Pallas kernels for 0% -> 0%
where the time goes in v1:
time: 860 us; the launch traced here: 852 us
  local copies, waits for them, and re-layouts  202 us (23%)
  other arithmetic  185 us (22%)
  matrix products  163 us (19%)
  waiting for transfers between devices  155 us (18%)
  blocking collectives  67.6 us (8%)
  starting transfers between devices  61.4 us (7%)
  between operations  17.1 us (2%)
    unnamed x232, local copies, waits for them, and re-layouts  53.7 us
    psum x1, waiting for transfers between devices, body(): early_summed = lax.psum(early_shards, 'ctx')  47.9 us
    unnamed x1, blocking collectives  33.7 us
    ppermute x12, waiting for transfers between devices, group_return(): back.append(lax.ppermute(parts[shift], 'ctx', pairs))  30.5 us
    psum x1, waiting for transfers between devices, body(): qkv_summed = lax.psum(qkv_shard, 'ctx')  25.4 us
    convert_element_type x1, other arithmetic, body(): d_scores = (probs * (d_probs - row_delta)).astype(jnp.bfloat16)  23.8 us
    ppermute x12, waiting for transfers between devices, group_send(): block = lax.ppermute(block, 'ctx', pairs)  19.5 us
    all_gather x1, waiting for transfers between devices, body(): packed_all = lax.all_gather(packed, 'shard', axis=0, tiled=False)  18.9 us
  transfers between devices with their start and end apart: 47, of which 21 were waited for; matrix products, arithmetic and copies ran while one was open for 53% of the time, Pallas kernels for 0%

profile of v1, /device:TPU:0, one launch (start us, length us, event | category | flops | bytes accessed | tf_op | source)
XLA Modules:
  0.0 851.8 jit_solution(3133075433952976300)
XLA Ops:
  9.6 15.1 %all-gather.1 = bf16[4,6,1024]{2,1,0:T(8,128)(2,1)S(1)} all-gather(bf16[1,6,1024]{2,1,0:T(8,128)(2,1)} %bitcast.398), channel_id=1, replica_groups=mesh['shard'=4,'ctx'=4,'tp'=2] {'shard'}, dimensions={0}, use_global_device_ids=true | all-gather | bytes 61440 | tf_op jit(solution)/shard_map/all_gather | solution.py:145
  29.9 33.7 %fusion = f32[8,6144]{1,0:T(8,128)S(1)} fusion(f32[24,6144]{1,0:T(8,128)} %fusion.65), kind=kCustom, calls=%all-reduce-scatter | all-reduce-scatter fusion | flops 196609 | bytes 786944
  63.6 4.5 collective-permute-start.37
  71.8 10.8 %pad_maximum_fusion = bf16[1179648]{0:T(1024)(128)(2,1)} fusion(bf16[524288]{0:T(1024)(128)(2,1)S(1)} %bitcast.365, bf16[524288]{0:T(1024)(128)(2,1)S(1)} %bitcast.364, bf16[131072]{0:T(1024)(128)(2,1)S(1)} %bitcast.375), kind=kLoop, calls=%fused_computation.87 | loop fusion | flops 7077888 | bytes 4718592 | tf_op jit(solution)/shard_map/concatenate | solution.py:130
  85.6 4.6 broadcast_compare_fusion
  97.4 6.3 fusion.27
  131.5 5.7 collective-permute-done.7
  139.6 4.9 collective-permute-done.5
  146.9 5.8 collective-permute-done.4
  153.9 17.3 %select_reduce_fusion = (f32[6,2,4,170]{3,2,1,0:T(4,128)S(1)}, f32[6,2,4,170,4,170]{3,5,4,2,1,0:T(8,128)}) fusion(pred[6,4,170,4,170]{2,4,3,1,0:T(8,128)(4,1)} %broadcast_compare_fusion, bf16[1,6,170,2,64]{2,4,0,3,1:T(8,128)(2,1)} %bitcast.37, bf16[1,6,170,2,64]{2,4,0,3,1:T(8,128)(2,1)} %bitcast.35, bf16[1,6,170,2,64]{2,4,0,3,1:T(8,128)(2,1)} %bitcast.33, ...), kind=kOutput, calls=%fused_computation.12 | convolution fusion | flops 729691648 | bytes 27091200 | tf_op jit(solution)/shard_map/amqgd,bmkgd->mgaqbk/dot_general | solution.py:184
  171.2 15.7 %fusion.3 = f32[6,2,4,170]{3,2,1,0:T(4,128)S(1)} fusion(f32[6,2,4,170,4,170]{3,5,4,2,1,0:T(8,128)} %get-tuple-element.186, f32[6,2,4,170]{3,2,1,0:T(4,128)S(1)} %get-tuple-element.185, pred[6,4,170,4,170]{2,4,3,1,0:T(8,128)(4,1)} %broadcast_compare_fusion), kind=kLoop, calls=%fused_computation.13 | loop fusion | flops 16638240 | bytes 25034880 | tf_op jit(solution)/shard_map/reduce_sum | solution.py:192
  187.0 6.7 copy-done
  193.7 12.2 %divide_convert_fusion = bf16[6,2,4,170,4,170]{3,5,4,2,1,0:T(8,128)(2,1)} fusion(f32[6,2,4,170,4,170]{3,5,4,2,1,0:T(8,128)S(1)} %copy-done, f32[6,2,4,170]{3,2,1,0:T(4,128)S(1)} %fusion.3, f32[6,2,4,170]{3,2,1,0:T(4,128)S(1)} %get-tuple-element.185, pred[6,4,170,4,170]{2,4,3,1,0:T(8,128)(4,1)} %broadcast_compare_fusion), kind=kLoop, calls=%fused_computation.10 | loop fusion | flops 22195200 | bytes 36132480 | tf_op jit(solution)/shard_map/convert_element_type | solution.py:194
  205.9 9.6 %fusion.35 = bf16[4,6,170,2,64]{2,4,0,3,1:T(8,128)(2,1)S(1)} fusion(bf16[6,2,4,170,4,170]{3,5,4,2,1,0:T(8,128)(2,1)} %divide_convert_fusion, bf16[1,6,170,2,64]{2,4,0,3,1:T(8,128)(2,1)} %bitcast.15, bf16[1,6,170,2,64]{2,4,0,3,1:T(8,128)(2,1)} %bitcast.13, bf16[1,6,170,2,64]{2,4,0,3,1:T(8,128)(2,1)} %bitcast.11, ...), kind=kOutput, calls=%fused_computation.107 | convolution fusion | flops 714946560 | bytes 13186560 | tf_op jit(solution)/shard_map/mgaqbk,bmkgd->amqgd/dot_general | solution.py:195
  224.6 4.1 mul.544
  228.8 5.3 collective-permute-done.11
  241.0 18.9 %all-gather.7.cloned.1.call-done = bf16[4718592]{0:T(1024)(128)(2,1)} async-done(((bf16[1179648]{0:T(1024)(128)(2,1)}), bf16[4718592]{0:T(1024)(128)(2,1)}) %all-gather.7.cloned.1.call-update) | async-done | bytes 9437200 | tf_op jit(solution)/shard_map/all_gather | solution.py:133
  259.9 12.5 %reshape.660 = bf16[4,1179648]{1,0:T(4,128)(2,1)} reshape(bf16[4718592]{0:T(1024)(128)(2,1)} %all-gather.7.cloned.1.call-done) | data formatting | bytes 18874368 | tf_op jit(solution)/shard_map/all_gather | solution.py:133
  278.0 8.3 fusion.72
  286.3 8.0 reshape_reshape.7
  294.3 4.8 copy.350
  299.2 6.3 copy.241
  305.5 9.2 %multiply_reduce_fusion.6 = (f32[]{:T(128)}, f32[1020,1024]{1,0:T(8,128)}) fusion(f32[1020,1024]{1,0:T(8,128)} %mul.544, f32[1024]{0:T(1024)S(1)} %copy-done.76, f32[1020,1024]{1,0:T(8,128)} %fusion.76, f32[1020,1024]{1,0:T(8,128)} %collective-permute-done.12), kind=kLoop, calls=%fused_computation.58 | loop fusion | flops 5222399 | bytes 16715780 | tf_op jit(solution)/shard_map/reduce_sum | solution.py:311
  314.7 4.3 reshape.590
  327.9 7.5 fusion.77
  335.4 10.6 %fusion.69 = (f32[2048]{0:T(1024)}, bf16[1020,2048]{1,0:T(8,128)(2,1)S(1)}) fusion(f32[1020,2048]{1,0:T(8,128)S(1)} %fusion.77, f32[2048]{0:T(1024)S(1)} %copy-done.97, bf16[1020,1024]{1,0:T(8,128)(2,1)S(1)} %copy-done.30, bf16[2048,1024]{0,1:T(8,128)(2,1)S(1)} %bitcast.360), kind=kOutput, calls=%fused_computation.245 | convolution fusion | flops 4324145152 | bytes 18833408 | tf_op jit(solution)/shard_map/rd,fd->rf/dot_general | solution.py:218
  346.1 6.1 fusion.32
  352.7 6.9 fusion.67
  362.2 4.1 mul.547
  366.3 6.8 add.471
  373.1 4.2 reshape.596
  377.4 9.3 %multiply_reduce_fusion.5 = (f32[]{:T(128)}, f32[1020,1024]{1,0:T(8,128)}) fusion(f32[1020,1024]{1,0:T(8,128)} %mul.547, f32[1024]{0:T(1024)S(1)} %copy-done.85, f32[1020,1024]{1,0:T(8,128)} %fusion.67, f32[1020,1024]{1,0:T(8,128)} %collective-permute-done.13), kind=kLoop, calls=%fused_computation.57 | loop fusion | flops 5222399 | bytes 16715780 | tf_op jit(solution)/shard_map/reduce_sum | solution.py:311
  386.7 4.3 reshape.594
  390.9 8.3 multiply_reduce_fusion
  399.3 3.5 multiply_reduce_fusion.1
  402.8 5.7 multiply_reduce_fusion.7
  413.1 4.0 convolution_convert_fusion.3
  417.1 8.3 convolution_convert_fusion.1
  442.6 11.9 %convolution_convert_fusion = bf16[2048,1024]{1,0:T(8,128)(2,1)} fusion(bf16[1020,1024]{1,0:T(8,128)(2,1)S(1)} %copy-done.31, f32[1020,2048]{1,0:T(8,128)} %copy-done.102, f32[2048]{0:T(1024)S(1)} %copy-done.98), kind=kOutput, calls=%fused_computation.65 | convolution fusion | flops 4301176832 | bytes 14647296 | tf_op jit(solution)/shard_map/rf,rd->fd/dot_general | solution.py:217
  459.8 11.7 %fusion.38 = bf16[4,6,170,2,64]{2,4,0,3,1:T(8,128)(2,1)S(1)} fusion(bf16[6,2,4,170,4,170]{3,5,4,2,1,0:T(8,128)(2,1)} %divide_convert_fusion, bf16[1,6,170,2,64]{2,4,0,3,1:T(8,128)(2,1)} %bitcast.373, bf16[1,6,170,2,64]{2,4,0,3,1:T(8,128)(2,1)S(1)} %bitcast.371, bf16[1,6,170,2,64]{2,4,0,3,1:T(8,128)(2,1)S(1)} %bitcast.369, ...), kind=kOutput, calls=%fused_computation.110 | convolution fusion | flops 714946560 | bytes 13186560 | tf_op jit(solution)/shard_map/mgaqbk,amqgd->bmkgd/dot_general | solution.py:248
  471.6 18.3 %fusion.1 = (f32[6,2,4,170]{3,2,1,0:T(4,128)S(1)}, f32[6,2,4,170,4,170]{3,5,4,2,1,0:T(8,128)}) fusion(bf16[6,2,4,170,4,170]{3,5,4,2,1,0:T(8,128)(2,1)} %divide_convert_fusion, bf16[1,6,170,2,64]{2,4,0,3,1:T(8,128)(2,1)} %bitcast.15, bf16[1,6,170,2,64]{2,4,0,3,1:T(8,128)(2,1)} %bitcast.13, bf16[1,6,170,2,64]{2,4,0,3,1:T(8,128)(2,1)} %bitcast.11, ...), kind=kOutput, calls=%fused_computation.8 | convolution fusion | flops 735240448 | bytes 35414400 | tf_op jit(solution)/shard_map/amqgd,bmkgd->mgaqbk/dot_general | solution.py:236
  494.4 23.8 %fusion.2 = bf16[6,2,4,170,4,170]{3,5,4,2,1,0:T(8,128)(2,1)S(1)} fusion(f32[6,2,4,170,4,170]{3,5,4,2,1,0:T(8,128)} %get-tuple-element.188, f32[6,2,4,170]{3,2,1,0:T(4,128)S(1)} %get-tuple-element.187, f32[6,2,4,170]{3,2,1,0:T(4,128)S(1)} %copy-done.55, f32[6,2,4,170]{3,2,1,0:T(4,128)S(1)} %copy-done.53, f32[6,2,4,170,4,170]{3,5,4,2,1,0:T(8,128)} %get-tuple-element.186, ...), kind=kLoop, calls=%fused_computation.9 | loop fusion | flops 44390400 | bytes 58360320 | tf_op jit(solution)/shard_map/convert_element_type | solution.py:240
  518.3 6.0 copy-done.1
  524.2 4.4 fusion.36
  528.6 12.4 %fusion.37 = bf16[4,6,170,2,64]{2,4,0,3,1:T(8,128)(2,1)S(1)} fusion(bf16[6,2,4,170,4,170]{3,5,4,2,1,0:T(8,128)(2,1)} %copy-done.1, bf16[1,6,170,2,64]{2,4,0,3,1:T(8,128)(2,1)} %bitcast.388, bf16[1,6,170,2,64]{2,4,0,3,1:T(8,128)(2,1)} %bitcast.390, bf16[1,6,170,2,64]{2,4,0,3,1:T(8,128)(2,1)} %bitcast.392, bf16[1,6,170,2,64]{2,4,0,3,1:T(8,128)(2,1)} %get-tuple-element.162), kind=kOutput, calls=%fused_computation.109 | convolution fusion | flops 714946560 | bytes 13186560 | tf_op jit(solution)/shard_map/mgaqbk,amqgd->bmkgd/dot_general | solution.py:245
  556.4 7.3 collective-permute-done.23
  571.7 7.1 collective-permute-done.20
  586.3 4.9 convert_bitcast_fusion.1
  634.7 9.1 %add_add_fusion.4 = (bf16[6,170,1,512]{3,1,2,0:T(8,128)(2,1)}, bf16[6,170,1,512]{3,1,2,0:T(8,128)(2,1)}) fusion(f32[6,170,1,512]{3,1,2,0:T(8,128)} %copy.255, f32[6,170,1,512]{3,1,2,0:T(8,128)} %copy.253, f32[6,170,1,512]{3,1,2,0:T(8,128)S(1)} %copy-done.18, f32[512]{0:T(512)S(1)} %copy-done.80, f32[512]{0:T(512)S(1)} %mul.506, ...), kind=kLoop, calls=%fused_computation.68 | loop fusion | flops 6266880 | bytes 18804736 | tf_op jit(solution)/shard_map/transpose(jvp())/add_any | solution.py:18
  654.3 7.0 fusion.78
  661.3 4.9 convolution_convert_fusion.2
  667.2 47.9 %all-reduce.9.cloned.1.call-done = (bf16[256,2048]{1,0:T(8,128)(2,1)}, bf16[512,256]{1,0:T(8,128)(2,1)}, bf16[2048,256]{1,0:T(8,128)(2,1)}) async-done(((bf16[256,2048]{1,0:T(8,128)(2,1)}, bf16[512,256]{1,0:T(8,128)(2,1)}, bf16[2048,256]{1,0:T(8,128)(2,1)}), (bf16[256,2048]{1,0:T(8,128)(2,1)}, bf16[512,256]{1,0:T(8,128)(2,1)}, bf16[2048,256]{1,0:T(8,128)(2,1)})) %all-reduce.9.cloned.1.call-update) | async-done | bytes 2359312 | tf_op jit(solution)/shard_map/psum | solution.py:300
  721.6 4.7 collective-permute-done.35
  728.6 6.9 add.475
  735.5 4.3 reshape.598
  739.8 3.5 fusion.68
  745.8 18.8 %all-reduce.10 = bf16[6,6,1024]{2,1,0:T(8,128)(2,1)S(1)} all-reduce(f32[6,6,1024]{2,1,0:T(8,128)S(1)} %stack.200), channel_id=1, replica_groups=mesh['shard'=4,'ctx'=4,'tp'=2] {'ctx'}, use_global_device_ids=true, to_apply=%region_24.26 | all-reduce | flops 36864 | bytes 221184 | tf_op jit(solution)/shard_map/psum | solution.py:276
  764.7 4.9 collective-permute-start.28
  774.8 5.4 collective-permute-start.29
  785.0 5.3 add_convert_fusion
  796.5 3.8 all-to-all-start
  800.3 4.4 fusion.66
  805.4 6.7 copy.279
  816.6 25.4 %all-reduce.7.cloned.1.call-done = bf16[256,3,512]{2,0,1:T(8,128)(2,1)} async-done(((bf16[256,3,512]{2,0,1:T(8,128)(2,1)}), bf16[256,3,512]{2,0,1:T(8,128)(2,1)}) %all-reduce.7.cloned.1.call-update) | async-done | bytes 786448 | tf_op jit(solution)/shard_map/psum | solution.py:303
  (471 shorter events, 239.4 us)
Async XLA Ops:
  7.2 90.3 %all-gather.5.cloned.1.call-start = ((), (), s32[]{:S(2)}) async-start(), calls=%async_computation.5 | async-start | bytes 3932160 | tf_op jit(solution)/shard_map/all_gather | solution.py:129
  9.5 250.4 %all-gather.7.cloned.1.call-start = ((), (), s32[]{:S(2)}) async-start(), calls=%async_computation.11 | async-start | bytes 11796480 | tf_op jit(solution)/shard_map/all_gather | solution.py:133
  28.0 42.7 %copy-start.11 = (bf16[256,6,1024]{0,2,1:T(8,128)(2,1)}, bf16[256,6,1024]{0,2,1:T(8,128)(2,1)S(1)}, u32[]{:S(2)}) copy-start(bf16[256,6,1024]{0,2,1:T(8,128)(2,1)S(1)} %copy.226) | copy-start | bytes 9437188
  63.6 29.0 %collective-permute-start.37 = (f32[6,6144]{1,0:T(8,128)S(1)}, f32[6,6144]{1,0:T(8,128)}, u32[]{:S(2)}, u32[]{:S(2)}) collective-permute-start(f32[6,6144]{1,0:T(8,128)S(1)} %slice.187), channel_id=1, source_target_pairs={{0,8},{8,16},{16,24},{1,9},{9,17},{17,25},{2,10},{10,18},{18,26},{... | collective-permute-start | bytes 442376
  82.6 561.1 %reduce-scatter.9.cloned.1.call-start = ((), (), s32[]{:S(2)}) async-start(), calls=%async_computation.7 | async-start | bytes 1310720 | tf_op jit(solution)/shard_map/reduce_scatter | solution.py:297
  90.4 32.7 %copy-start.72 = (f32[4,2,64]{2,1,0:T(2,128)}, f32[4,2,64]{2,1,0:T(2,128)S(1)}, u32[]{:S(2)}) copy-start(f32[4,2,64]{2,1,0:T(2,128)S(1)} %add.444) | copy-start | bytes 6148
  90.5 30.9 %copy-start.74 = (f32[8,64]{1,0:T(8,128)}, f32[8,64]{1,0:T(8,128)S(1)}, u32[]{:S(2)}) copy-start(f32[8,64]{1,0:T(8,128)S(1)} %add.447) | copy-start | bytes 6148
  90.6 32.5 %copy-start.81 = (f32[4,2]{1,0:T(4,128)}, f32[4,2]{1,0:T(4,128)S(1)}, u32[]{:S(2)}) copy-start(f32[4,2]{1,0:T(4,128)S(1)} %mul.464) | copy-start | bytes 100
  115.3 13.1 %collective-permute-start.8 = (bf16[6,170,2,64]{1,3,2,0:T(8,128)(2,1)}, bf16[6,170,2,64]{1,3,2,0:T(8,128)(2,1)}, u32[]{:S(2)}, u32[]{:S(2)}) collective-permute-start(bf16[6,170,2,64]{1,3,2,0:T(8,128)(2,1)} %get-tuple-element.167), channel_id=1, source_target_pairs={{0,6},{2,0},{4,2},{6,4},{1,7},{3,1},{5,3},{7,5},{8,14},{10,8},{12,... | collective-permute-start | bytes 783368 | tf_op jit(solution)/shard_map/ppermute | solution.py:63
  117.8 19.4 %collective-permute-start.7 = (bf16[6,170,2,64]{1,3,2,0:T(8,128)(2,1)}, bf16[6,170,2,64]{1,3,2,0:T(8,128)(2,1)}, u32[]{:S(2)}, u32[]{:S(2)}) collective-permute-start(bf16[6,170,2,64]{1,3,2,0:T(8,128)(2,1)} %get-tuple-element.168), channel_id=1, source_target_pairs={{0,4},{2,6},{4,0},{6,2},{1,5},{3,7},{5,1},{7,3},{8,12},{10,14},{12... | collective-permute-start | bytes 783368 | tf_op jit(solution)/shard_map/ppermute | solution.py:63
  118.3 20.8 %collective-permute-start.6 = (bf16[6,170,2,64]{1,3,2,0:T(8,128)(2,1)}, bf16[6,170,2,64]{1,3,2,0:T(8,128)(2,1)}, u32[]{:S(2)}, u32[]{:S(2)}) collective-permute-start(bf16[6,170,2,64]{1,3,2,0:T(8,128)(2,1)} %get-tuple-element.169), channel_id=1, source_target_pairs={{0,2},{2,4},{4,6},{6,0},{1,3},{3,5},{5,7},{7,1},{8,10},{10,12},{12... | collective-permute-start | bytes 783368 | tf_op jit(solution)/shard_map/ppermute | solution.py:63
  124.6 19.9 %collective-permute-start.5 = (bf16[6,170,2,64]{1,3,2,0:T(8,128)(2,1)S(1)}, bf16[6,170,2,64]{1,3,2,0:T(8,128)(2,1)S(1)}, u32[]{:S(2)}, u32[]{:S(2)}) collective-permute-start(bf16[6,170,2,64]{1,3,2,0:T(8,128)(2,1)S(1)} %get-tuple-element.163), channel_id=1, source_target_pairs={{0,6},{2,0},{4,2},{6,4},{1,7},{3,1},{5,3},{7,5},{8,14},{10,8},{12,... | collective-permute-start | bytes 783368 | tf_op jit(solution)/shard_map/ppermute | solution.py:63
  126.9 25.8 %collective-permute-start.4 = (bf16[6,170,2,64]{1,3,2,0:T(8,128)(2,1)S(1)}, bf16[6,170,2,64]{1,3,2,0:T(8,128)(2,1)S(1)}, u32[]{:S(2)}, u32[]{:S(2)}) collective-permute-start(bf16[6,170,2,64]{1,3,2,0:T(8,128)(2,1)S(1)} %get-tuple-element.164), channel_id=1, source_target_pairs={{0,4},{2,6},{4,0},{6,2},{1,5},{3,7},{5,1},{7,3},{8,12},{10,14},{12... | collective-permute-start | bytes 783368 | tf_op jit(solution)/shard_map/ppermute | solution.py:63
  128.4 25.5 %collective-permute-start.3 = (bf16[6,170,2,64]{1,3,2,0:T(8,128)(2,1)S(1)}, bf16[6,170,2,64]{1,3,2,0:T(8,128)(2,1)S(1)}, u32[]{:S(2)}, u32[]{:S(2)}) collective-permute-start(bf16[6,170,2,64]{1,3,2,0:T(8,128)(2,1)S(1)} %get-tuple-element.165), channel_id=1, source_target_pairs={{0,2},{2,4},{4,6},{6,0},{1,3},{3,5},{5,7},{7,1},{8,10},{10,12},{12... | collective-permute-start | bytes 783368 | tf_op jit(solution)/shard_map/ppermute | solution.py:63
  130.1 23.8 %copy-start.35 = (bf16[1,6,170,2,64]{2,4,0,3,1:T(8,128)(2,1)S(1)}, bf16[1,6,170,2,64]{2,4,0,3,1:T(8,128)(2,1)}, u32[]{:S(2)}) copy-start(bf16[1,6,170,2,64]{2,4,0,3,1:T(8,128)(2,1)} %get-tuple-element.166) | copy-start | bytes 783364
  130.1 23.8 %copy-start.37 = (bf16[1,6,170,2,64]{2,4,0,3,1:T(8,128)(2,1)S(1)}, bf16[1,6,170,2,64]{2,4,0,3,1:T(8,128)(2,1)}, u32[]{:S(2)}) copy-start(bf16[1,6,170,2,64]{2,4,0,3,1:T(8,128)(2,1)} %get-tuple-element.162) | copy-start | bytes 783364
  131.5 74.4 %copy-start.26 = (bf16[1,6,170,2,64]{2,4,0,3,1:T(8,128)(2,1)}, bf16[1,6,170,2,64]{2,4,0,3,1:T(8,128)(2,1)S(1)}, u32[]{:S(2)}) copy-start(bf16[1,6,170,2,64]{2,4,0,3,1:T(8,128)(2,1)S(1)} %get-tuple-element.158) | copy-start | bytes 783364
  137.2 68.7 %collective-permute-start.2 = (bf16[6,170,2,64]{1,3,2,0:T(8,128)(2,1)}, bf16[6,170,2,64]{1,3,2,0:T(8,128)(2,1)}, u32[]{:S(2)}, u32[]{:S(2)}) collective-permute-start(bf16[6,170,2,64]{1,3,2,0:T(8,128)(2,1)} %get-tuple-element.159), channel_id=1, source_target_pairs={{0,6},{2,0},{4,2},{6,4},{1,7},{3,1},{5,3},{7,5},{8,14},{10,8},{12,... | collective-permute-start | bytes 783368 | tf_op jit(solution)/shard_map/ppermute | solution.py:63
  139.0 66.8 %collective-permute-start.1 = (bf16[6,170,2,64]{1,3,2,0:T(8,128)(2,1)}, bf16[6,170,2,64]{1,3,2,0:T(8,128)(2,1)}, u32[]{:S(2)}, u32[]{:S(2)}) collective-permute-start(bf16[6,170,2,64]{1,3,2,0:T(8,128)(2,1)} %get-tuple-element.160), channel_id=1, source_target_pairs={{0,4},{2,6},{4,0},{6,2},{1,5},{3,7},{5,1},{7,3},{8,12},{10,14},{12... | collective-permute-start | bytes 783368 | tf_op jit(solution)/shard_map/ppermute | solution.py:63
  144.4 26.8 %copy-start.56 = (bf16[6,170,2,64]{1,3,2,0:T(8,128)(2,1)}, bf16[6,170,2,64]{1,3,2,0:T(8,128)(2,1)S(1)}, u32[]{:S(2)}) copy-start(bf16[6,170,2,64]{1,3,2,0:T(8,128)(2,1)S(1)} %collective-permute-done.5) | copy-start | bytes 783364
  144.4 61.4 %collective-permute-start = (bf16[6,170,2,64]{1,3,2,0:T(8,128)(2,1)}, bf16[6,170,2,64]{1,3,2,0:T(8,128)(2,1)}, u32[]{:S(2)}, u32[]{:S(2)}) collective-permute-start(bf16[6,170,2,64]{1,3,2,0:T(8,128)(2,1)} %get-tuple-element.161), channel_id=1, source_target_pairs={{0,2},{2,4},{4,6},{6,0},{1,3},{3,5},{5,7},{7,1},{8,10},{10,12},{12... | collective-permute-start | bytes 783368 | tf_op jit(solution)/shard_map/ppermute | solution.py:63
  152.7 18.5 %copy-start.57 = (bf16[6,170,2,64]{1,3,2,0:T(8,128)(2,1)}, bf16[6,170,2,64]{1,3,2,0:T(8,128)(2,1)S(1)}, u32[]{:S(2)}) copy-start(bf16[6,170,2,64]{1,3,2,0:T(8,128)(2,1)S(1)} %collective-permute-done.4) | copy-start | bytes 783364
  153.9 17.3 %copy-start.58 = (bf16[6,170,2,64]{1,3,2,0:T(8,128)(2,1)}, bf16[6,170,2,64]{1,3,2,0:T(8,128)(2,1)S(1)}, u32[]{:S(2)}) copy-start(bf16[6,170,2,64]{1,3,2,0:T(8,128)(2,1)S(1)} %collective-permute-done.3) | copy-start | bytes 783364
  171.2 15.8 %copy-start.52 = (f32[6,2,4,170]{3,2,1,0:T(4,128)}, f32[6,2,4,170]{3,2,1,0:T(4,128)S(1)}, u32[]{:S(2)}) copy-start(f32[6,2,4,170]{3,2,1,0:T(4,128)S(1)} %get-tuple-element.185) | copy-start | bytes 97924
  171.2 22.4 %copy-start = (f32[6,2,4,170,4,170]{3,5,4,2,1,0:T(8,128)S(1)}, f32[6,2,4,170,4,170]{3,5,4,2,1,0:T(8,128)}, u32[]{:S(2)}) copy-start(f32[6,2,4,170,4,170]{3,5,4,2,1,0:T(8,128)} %get-tuple-element.186) | copy-start | bytes 66585604
  216.5 12.3 %collective-permute-start.9 = (bf16[6,170,2,64]{1,3,2,0:T(8,128)(2,1)}, bf16[6,170,2,64]{1,3,2,0:T(8,128)(2,1)S(1)}, u32[]{:S(2)}, u32[]{:S(2)}) collective-permute-start(bf16[6,170,2,64]{1,3,2,0:T(8,128)(2,1)} %get-tuple-element.155), channel_id=1, source_target_pairs={{0,6},{2,0},{4,2},{6,4},{1,7},{3,1},{5,3},{7,5},{8,14},{10,8},{12,... | collective-permute-start | bytes 783368 | tf_op jit(solution)/shard_map/ppermute | solution.py:74
  218.5 15.5 %collective-permute-start.11 = (bf16[6,170,2,64]{1,3,2,0:T(8,128)(2,1)}, bf16[6,170,2,64]{1,3,2,0:T(8,128)(2,1)}, u32[]{:S(2)}, u32[]{:S(2)}) collective-permute-start(bf16[6,170,2,64]{1,3,2,0:T(8,128)(2,1)} %get-tuple-element.156), channel_id=1, source_target_pairs={{0,2},{2,4},{4,6},{6,0},{1,3},{3,5},{5,7},{7,1},{8,10},{10,12},{12... | collective-permute-start | bytes 783368 | tf_op jit(solution)/shard_map/ppermute | solution.py:74
  218.7 16.8 %collective-permute-start.10 = (bf16[6,170,2,64]{1,3,2,0:T(8,128)(2,1)S(1)}, bf16[6,170,2,64]{1,3,2,0:T(8,128)(2,1)}, u32[]{:S(2)}, u32[]{:S(2)}) collective-permute-start(bf16[6,170,2,64]{1,3,2,0:T(8,128)(2,1)S(1)} %get-tuple-element.157), channel_id=1, source_target_pairs={{0,4},{2,6},{4,0},{6,2},{1,5},{3,7},{5,1},{7,3},{8,12},{10,14},{12... | collective-permute-start | bytes 783368 | tf_op jit(solution)/shard_map/ppermute | solution.py:74
  278.0 27.5 %collective-permute-start.12 = (f32[1020,1024]{1,0:T(8,128)}, f32[1020,1024]{1,0:T(8,128)}, u32[]{:S(2)}, u32[]{:S(2)}) collective-permute-start(f32[1020,1024]{1,0:T(8,128)} %fusion.76), channel_id=1, source_target_pairs={{0,1},{1,0},{2,3},{3,2},{4,5},{5,4},{6,7},{7,6},{8,9},{9,8},{10,11... | collective-permute-start | bytes 12533768 | tf_op jit(solution)/shard_map/ppermute | solution.py:34
  335.4 17.4 %copy-start.102 = (f32[1020,2048]{1,0:T(8,128)}, f32[1020,2048]{1,0:T(8,128)S(1)}, u32[]{:S(2)}) copy-start(f32[1020,2048]{1,0:T(8,128)S(1)} %fusion.77) | copy-start | bytes 25067524
  352.2 14.1 %collective-permute-start.14 = (f32[1020,1024]{1,0:T(8,128)}, f32[1020,1024]{1,0:T(8,128)}, u32[]{:S(2)}, u32[]{:S(2)}) collective-permute-start(f32[1020,1024]{1,0:T(8,128)} %fusion.32), channel_id=1, source_target_pairs={{0,1},{1,0},{2,3},{3,2},{4,5},{5,4},{6,7},{7,6},{8,9},{9,8},{10,11... | collective-permute-start | bytes 12533768 | tf_op jit(solution)/shard_map/ppermute | solution.py:34
  359.7 17.7 %collective-permute-start.13 = (f32[1020,1024]{1,0:T(8,128)}, f32[1020,1024]{1,0:T(8,128)}, u32[]{:S(2)}, u32[]{:S(2)}) collective-permute-start(f32[1020,1024]{1,0:T(8,128)} %fusion.67), channel_id=1, source_target_pairs={{0,1},{1,0},{2,3},{3,2},{4,5},{5,4},{6,7},{7,6},{8,9},{9,8},{10,11... | collective-permute-start | bytes 12533768 | tf_op jit(solution)/shard_map/ppermute | solution.py:34
  417.1 226.7 %reduce-scatter.7.cloned.1.call-start = ((), (), s32[]{:S(2)}) async-start(), calls=%async_computation.6 | async-start | bytes 5242880 | tf_op jit(solution)/shard_map/reduce_scatter | solution.py:296
  425.5 218.3 %reduce-scatter.11.cloned.1.call-start = ((), (), s32[]{:S(2)}) async-start(), calls=%async_computation.8 | async-start | bytes 5242880 | tf_op jit(solution)/shard_map/reduce_scatter | solution.py:298
  438.2 19.0 %collective-permute-start.15 = (bf16[6,170,2,64]{1,3,2,0:T(8,128)(2,1)S(1)}, bf16[6,170,2,64]{1,3,2,0:T(8,128)(2,1)S(1)}, u32[]{:S(2)}, u32[]{:S(2)}) collective-permute-start(bf16[6,170,2,64]{1,3,2,0:T(8,128)(2,1)S(1)} %bitcast.382), channel_id=1, source_target_pairs={{0,2},{2,4},{4,6},{6,0},{1,3},{3,5},{5,7},{7,1},{8,10},{10,12},{12... | collective-permute-start | bytes 783368 | tf_op jit(solution)/shard_map/ppermute | solution.py:63
  439.7 19.3 %collective-permute-start.16 = (bf16[6,170,2,64]{1,3,2,0:T(8,128)(2,1)S(1)}, bf16[6,170,2,64]{1,3,2,0:T(8,128)(2,1)S(1)}, u32[]{:S(2)}, u32[]{:S(2)}) collective-permute-start(bf16[6,170,2,64]{1,3,2,0:T(8,128)(2,1)S(1)} %bitcast.381), channel_id=1, source_target_pairs={{0,4},{2,6},{4,0},{6,2},{1,5},{3,7},{5,1},{7,3},{8,12},{10,14},{12... | collective-permute-start | bytes 783368 | tf_op jit(solution)/shard_map/ppermute | solution.py:63
  441.2 17.9 %collective-permute-start.17 = (bf16[6,170,2,64]{1,3,2,0:T(8,128)(2,1)S(1)}, bf16[6,170,2,64]{1,3,2,0:T(8,128)(2,1)S(1)}, u32[]{:S(2)}, u32[]{:S(2)}) collective-permute-start(bf16[6,170,2,64]{1,3,2,0:T(8,128)(2,1)S(1)} %bitcast.380), channel_id=1, source_target_pairs={{0,6},{2,0},{4,2},{6,4},{1,7},{3,1},{5,3},{7,5},{8,14},{10,8},{12,... | collective-permute-start | bytes 783368 | tf_op jit(solution)/shard_map/ppermute | solution.py:63
  454.5 260.6 %all-reduce.9.cloned.1.call-start = ((), (), s32[]{:S(2)}) async-start(), calls=%async_computation.12 | async-start | bytes 4718592 | tf_op jit(solution)/shard_map/psum | solution.py:300
  491.0 55.1 %collective-permute-start.24 = (bf16[6,170,2,64]{1,3,2,0:T(8,128)(2,1)}, bf16[6,170,2,64]{1,3,2,0:T(8,128)(2,1)}, u32[]{:S(2)}, u32[]{:S(2)}) collective-permute-start(bf16[6,170,2,64]{1,3,2,0:T(8,128)(2,1)} %get-tuple-element.151), channel_id=1, source_target_pairs={{0,6},{2,0},{4,2},{6,4},{1,7},{3,1},{5,3},{7,5},{8,14},{10,8},{12,... | collective-permute-start | bytes 783368 | tf_op jit(solution)/shard_map/ppermute | solution.py:74
  492.6 54.0 %collective-permute-start.26 = (bf16[6,170,2,64]{1,3,2,0:T(8,128)(2,1)}, bf16[6,170,2,64]{1,3,2,0:T(8,128)(2,1)}, u32[]{:S(2)}, u32[]{:S(2)}) collective-permute-start(bf16[6,170,2,64]{1,3,2,0:T(8,128)(2,1)} %get-tuple-element.152), channel_id=1, source_target_pairs={{0,2},{2,4},{4,6},{6,0},{1,3},{3,5},{5,7},{7,1},{8,10},{10,12},{12... | collective-permute-start | bytes 783368 | tf_op jit(solution)/shard_map/ppermute | solution.py:74
  493.0 56.5 %collective-permute-start.25 = (bf16[6,170,2,64]{1,3,2,0:T(8,128)(2,1)}, bf16[6,170,2,64]{1,3,2,0:T(8,128)(2,1)}, u32[]{:S(2)}, u32[]{:S(2)}) collective-permute-start(bf16[6,170,2,64]{1,3,2,0:T(8,128)(2,1)} %get-tuple-element.153), channel_id=1, source_target_pairs={{0,4},{2,6},{4,0},{6,2},{1,5},{3,7},{5,1},{7,3},{8,12},{10,14},{12... | collective-permute-start | bytes 783368 | tf_op jit(solution)/shard_map/ppermute | solution.py:74
  494.4 29.8 %copy-start.36 = (bf16[1,6,170,2,64]{2,4,0,3,1:T(8,128)(2,1)S(1)}, bf16[1,6,170,2,64]{2,4,0,3,1:T(8,128)(2,1)}, u32[]{:S(2)}) copy-start(bf16[1,6,170,2,64]{2,4,0,3,1:T(8,128)(2,1)} %get-tuple-element.166) | copy-start | bytes 783364
  542.2 12.6 %collective-permute-start.21 = (bf16[6,170,2,64]{1,3,2,0:T(8,128)(2,1)}, bf16[6,170,2,64]{1,3,2,0:T(8,128)(2,1)}, u32[]{:S(2)}, u32[]{:S(2)}) collective-permute-start(bf16[6,170,2,64]{1,3,2,0:T(8,128)(2,1)} %get-tuple-element.147), channel_id=1, source_target_pairs={{0,6},{2,0},{4,2},{6,4},{1,7},{3,1},{5,3},{7,5},{8,14},{10,8},{12,... | collective-permute-start | bytes 783368 | tf_op jit(solution)/shard_map/ppermute | solution.py:74
  546.1 17.6 %collective-permute-start.23 = (bf16[6,170,2,64]{1,3,2,0:T(8,128)(2,1)}, bf16[6,170,2,64]{1,3,2,0:T(8,128)(2,1)}, u32[]{:S(2)}, u32[]{:S(2)}) collective-permute-start(bf16[6,170,2,64]{1,3,2,0:T(8,128)(2,1)} %get-tuple-element.148), channel_id=1, source_target_pairs={{0,2},{2,4},{4,6},{6,0},{1,3},{3,5},{5,7},{7,1},{8,10},{10,12},{12... | collective-permute-start | bytes 783368 | tf_op jit(solution)/shard_map/ppermute | solution.py:74
  546.1 20.8 %collective-permute-start.22 = (bf16[6,170,2,64]{1,3,2,0:T(8,128)(2,1)}, bf16[6,170,2,64]{1,3,2,0:T(8,128)(2,1)}, u32[]{:S(2)}, u32[]{:S(2)}) collective-permute-start(bf16[6,170,2,64]{1,3,2,0:T(8,128)(2,1)} %get-tuple-element.149), channel_id=1, source_target_pairs={{0,4},{2,6},{4,0},{6,2},{1,5},{3,7},{5,1},{7,3},{8,12},{10,14},{12... | collective-permute-start | bytes 783368 | tf_op jit(solution)/shard_map/ppermute | solution.py:74
  546.7 25.0 %collective-permute-start.18 = (bf16[6,170,2,64]{1,3,2,0:T(8,128)(2,1)}, bf16[6,170,2,64]{1,3,2,0:T(8,128)(2,1)}, u32[]{:S(2)}, u32[]{:S(2)}) collective-permute-start(bf16[6,170,2,64]{1,3,2,0:T(8,128)(2,1)} %get-tuple-element.143), channel_id=1, source_target_pairs={{0,6},{2,0},{4,2},{6,4},{1,7},{3,1},{5,3},{7,5},{8,14},{10,8},{12,... | collective-permute-start | bytes 783368 | tf_op jit(solution)/shard_map/ppermute | solution.py:74
  549.5 29.3 %collective-permute-start.20 = (bf16[6,170,2,64]{1,3,2,0:T(8,128)(2,1)}, bf16[6,170,2,64]{1,3,2,0:T(8,128)(2,1)}, u32[]{:S(2)}, u32[]{:S(2)}) collective-permute-start(bf16[6,170,2,64]{1,3,2,0:T(8,128)(2,1)} %get-tuple-element.144), channel_id=1, source_target_pairs={{0,2},{2,4},{4,6},{6,0},{1,3},{3,5},{5,7},{7,1},{8,10},{10,12},{12... | collective-permute-start | bytes 783368 | tf_op jit(solution)/shard_map/ppermute | solution.py:74
  554.8 26.5 %collective-permute-start.19 = (bf16[6,170,2,64]{1,3,2,0:T(8,128)(2,1)}, bf16[6,170,2,64]{1,3,2,0:T(8,128)(2,1)}, u32[]{:S(2)}, u32[]{:S(2)}) collective-permute-start(bf16[6,170,2,64]{1,3,2,0:T(8,128)(2,1)} %get-tuple-element.145), channel_id=1, source_target_pairs={{0,4},{2,6},{4,0},{6,2},{1,5},{3,7},{5,1},{7,3},{8,12},{10,14},{12... | collective-permute-start | bytes 783368 | tf_op jit(solution)/shard_map/ppermute | solution.py:74
  566.8 14.5 %copy-start.34 = (bf16[1,6,170,2,64]{2,4,3,1,0:T(8,128)(2,1)S(1)}, bf16[1,6,170,2,64]{2,4,3,1,0:T(8,128)(2,1)}, u32[]{:S(2)}) copy-start(bf16[1,6,170,2,64]{2,4,3,1,0:T(8,128)(2,1)} %get-tuple-element.142) | copy-start | bytes 783364
  610.7 55.6 %collective-permute-start.33 = (f32[5131]{0:T(1024)S(1)}, f32[5131]{0:T(1024)S(1)}, u32[]{:S(2)}, u32[]{:S(2)}) collective-permute-start(f32[5131]{0:T(1024)S(1)} %concatenate.7), channel_id=1, source_target_pairs={{0,6},{2,0},{4,2},{6,4},{1,7},{3,1},{5,3},{7,5},{8,14},{10,8},{12,... | collective-permute-start | bytes 61580 | tf_op jit(solution)/shard_map/ppermute | solution.py:86
  610.8 55.5 %collective-permute-start.32 = (f32[5131]{0:T(1024)S(1)}, f32[5131]{0:T(1024)S(1)}, u32[]{:S(2)}, u32[]{:S(2)}) collective-permute-start(f32[5131]{0:T(1024)S(1)} %concatenate.7), channel_id=1, source_target_pairs={{0,4},{2,6},{4,0},{6,2},{1,5},{3,7},{5,1},{7,3},{8,12},{10,14},{12... | collective-permute-start | bytes 61580 | tf_op jit(solution)/shard_map/ppermute | solution.py:86
  611.4 55.0 %collective-permute-start.31 = (f32[5131]{0:T(1024)S(1)}, f32[5131]{0:T(1024)S(1)}, u32[]{:S(2)}, u32[]{:S(2)}) collective-permute-start(f32[5131]{0:T(1024)S(1)} %concatenate.7), channel_id=1, source_target_pairs={{0,2},{2,4},{4,6},{6,0},{1,3},{3,5},{5,7},{7,1},{8,10},{10,12},{12... | collective-permute-start | bytes 61580 | tf_op jit(solution)/shard_map/ppermute | solution.py:86
  643.8 149.6 %reduce-scatter.13.cloned.1.call-start = ((), (), s32[]{:S(2)}) async-start(), calls=%async_computation.9 | async-start | bytes 3932160 | tf_op jit(solution)/shard_map/reduce_scatter | solution.py:302
  661.3 67.3 %collective-permute-start.27 = (f32[1020,1024]{1,0:T(8,128)}, f32[1020,1024]{1,0:T(8,128)}, u32[]{:S(2)}, u32[]{:S(2)}) collective-permute-start(f32[1020,1024]{1,0:T(8,128)} %fusion.78), channel_id=1, source_target_pairs={{0,1},{1,0},{2,3},{3,2},{4,5},{5,4},{6,7},{7,6},{8,9},{9,8},{10,11... | collective-permute-start | bytes 12533768 | tf_op jit(solution)/shard_map/ppermute | solution.py:34
  666.3 48.9 %copy-start.93 = (pred[4]{0:T(512)(128)(4,1)S(1)}, pred[4]{0:T(512)(128)(4,1)}, u32[]{:S(2)}) copy-start(pred[4]{0:T(512)(128)(4,1)} %get-tuple-element.190) | copy-start | bytes 16
  666.3 60.8 %copy-start.95 = (pred[4]{0:T(512)(128)(4,1)S(1)}, pred[4]{0:T(512)(128)(4,1)}, u32[]{:S(2)}) copy-start(pred[4]{0:T(512)(128)(4,1)} %compare_and_fusion.2) | copy-start | bytes 16
  715.1 126.8 %all-reduce.7.cloned.1.call-start = ((), (), s32[]{:S(2)}) async-start(), calls=%async_computation.10 | async-start | bytes 1572864 | tf_op jit(solution)/shard_map/psum | solution.py:303
  715.3 6.3 collective-permute-start.36
  718.7 7.6 collective-permute-start.35
  718.7 7.6 collective-permute-start.34
  764.7 10.2 %collective-permute-start.28 = (bf16[6,6144]{1,0:T(8,128)(2,1)S(1)}, bf16[6,6144]{1,0:T(8,128)(2,1)S(1)}, u32[]{:S(2)}, u32[]{:S(2)}) collective-permute-start(bf16[6,6144]{1,0:T(8,128)(2,1)S(1)} %bitcast.384), channel_id=1, source_target_pairs={{0,8},{8,16},{16,24},{24,0},{1,9},{9,17},{17,25},{25,1},{2,10},{10... | collective-permute-start | bytes 221192 | tf_op jit(solution)/shard_map/ppermute | solution.py:284
  774.8 8.7 %collective-permute-start.29 = (bf16[6,6144]{1,0:T(8,128)(2,1)S(1)}, bf16[6,6144]{1,0:T(8,128)(2,1)S(1)}, u32[]{:S(2)}, u32[]{:S(2)}) collective-permute-start(bf16[6,6144]{1,0:T(8,128)(2,1)S(1)} %collective-permute-done.28), channel_id=1, source_target_pairs={{0,8},{8,16},{16,24},{24,0},{1,9},{9,17},{17,25},{25,1},{2,10},{10... | collective-permute-start | bytes 221192 | tf_op jit(solution)/shard_map/ppermute | solution.py:284
  783.5 8.9 %collective-permute-start.30 = (bf16[6,6144]{1,0:T(8,128)(2,1)S(1)}, bf16[6,6144]{1,0:T(8,128)(2,1)S(1)}, u32[]{:S(2)}, u32[]{:S(2)}) collective-permute-start(bf16[6,6144]{1,0:T(8,128)(2,1)S(1)} %collective-permute-done.29), channel_id=1, source_target_pairs={{0,8},{8,16},{16,24},{24,0},{1,9},{9,17},{17,25},{25,1},{2,10},{10... | collective-permute-start | bytes 221192 | tf_op jit(solution)/shard_map/ppermute | solution.py:284
  796.5 15.5 %all-to-all-start = ((f32[4,6,256]{2,1,0:T(8,128)}), f32[4,6,256]{2,1,0:T(8,128)S(1)}, u32[]{:S(2)}, u32[]{:S(2)}) async-start(f32[4,6,256]{2,1,0:T(8,128)} %fusion.79), calls=%async_computation | async-start | bytes 65536 | tf_op jit(solution)/shard_map/all_to_all | solution.py:292
  (88 other events, 425.1 us)
Sparse Core Ops, SparseCore 0:
  10.1 78.9 all-gather.4
  90.7 169.1 all-gather.6
  417.2 25.5 reduce-scatter.8
  445.0 75.2 reduce-scatter.6
  522.4 77.2 reduce-scatter.10
  643.9 71.1 all-reduce.8
  717.4 63.6 reduce-scatter.12
  793.5 48.4 all-reduce.6
